TPU v7x, 512 devices: a whole 4x4x16 slice. The times are simulated.
512 devices in a mesh: ep: 128 (over z, x, core), rep: 4 (over y).
Axes of the slice: x: 4, y: 4, z: 16, core: 2. Of those that a mesh axis runs over, the one named last changes fastest.
Arguments:
- tokens: bfloat16 [65536, 2048], P(('ep', 'rep')), may hold values from -6 to 6
- cotangent: bfloat16 [65536, 2048], P(('ep', 'rep')), may hold values from -6 to 6
- expert_ids: int32 [65536, 2], P(('ep', 'rep')), may hold values from 0 to 63, all different within a row; in each aligned block of 128 rows (0 to 127, 128 to 255, ...) at most 5 rows name the same one
- gate_values: float32 [65536, 2], P(('ep', 'rep')), may hold values from 0.1 to 1
- up_weight: bfloat16 [2048, 81920], P('rep', 'ep'), may hold values from -0.125 to 0.125
- down_weight: bfloat16 [81920, 2048], P('ep', 'rep'), may hold values from -0.15625 to 0.15625
Outputs:
- token_grad: bfloat16 [65536, 2048], P(('ep', 'rep'))
- gate_grad: float32 [65536, 2], P(('ep', 'rep'))
- down_grad: bfloat16 [81920, 2048], P('ep', 'rep')
Inputs may be any that keep to these rules, and one draw needn't show every extreme that they name: `expert_ids`: each token names two different experts; among the 256 assignments of one device's tokens at most 5 name the same expert, a bound that is reached in some blocks.
All inputs are finite; a program needn't handle non-finite values.
Results may differ from a plain program's by a relative error of at most 0.02.
Values may be sent and summed in bfloat16 or wider, within the bound.
No kernel may reach another device: no remote copies, remote signals or barrier semaphores. Data moves between devices by JAX's collectives and lax.ppermute only.
A program may use at most 128 MiB of HBM per device.

v0:
```python
import math

import jax
import jax.numpy as jnp
from jax import lax
from jax.sharding import PartitionSpec as P

tanh_scale = math.sqrt(2.0 / math.pi)
cubic_coef = 0.044715


def gelu_tanh(argument):
    inner_arg = tanh_scale * (argument + cubic_coef * argument * argument * argument)
    return 0.5 * argument * (1.0 + jnp.tanh(inner_arg))


def gelu_slope(argument):
    tanh_value = jnp.tanh(tanh_scale * (argument + cubic_coef * argument * argument * argument))
    return 0.5 * (1.0 + tanh_value) + 0.5 * argument * (
        1.0 - tanh_value * tanh_value
    ) * tanh_scale * (1.0 + 3.0 * cubic_coef * argument * argument)


def expert_terms(rows_x, rows_dy, rows_gate, up_weight, down_weight):
    contract_last = (((1,), (1,)), ((), ()))
    up_full = lax.all_gather(up_weight, "rep", axis=0, tiled=True)
    pre_act = jnp.dot(rows_x, up_full, preferred_element_type=jnp.float32)
    grad_hidden = lax.dot_general(
        rows_dy,
        lax.all_gather(down_weight, "rep", axis=1, tiled=True),
        contract_last,
        preferred_element_type=jnp.float32,
    )
    hidden = gelu_tanh(pre_act)
    hidden_bf = hidden.astype(jnp.bfloat16)
    gate_part = jnp.sum(hidden * grad_hidden, axis=1)
    scaled_dy = (rows_gate[:, None] * rows_dy.astype(jnp.float32)).astype(jnp.bfloat16)
    down_term = lax.dot_general(
        hidden_bf, scaled_dy, (((0,), (0,)), ((), ())), preferred_element_type=jnp.float32
    ).astype(jnp.bfloat16)
    down_sum = (
        lax.psum_scatter(down_term, "rep", scatter_dimension=1, tiled=True)
        .astype(jnp.float32)
        .astype(jnp.bfloat16)
    )
    grad_pre = (rows_gate[:, None] * grad_hidden * gelu_slope(pre_act)).astype(jnp.bfloat16)
    token_part = lax.dot_general(
        grad_pre, up_full, contract_last, preferred_element_type=jnp.float32
    ).astype(jnp.bfloat16)
    return (token_part, gate_part, down_sum)


def duplicate(array, owners):
    widened = jnp.broadcast_to(array[:, None], (array.shape[0], 2) + array.shape[1:])
    return widened.reshape((owners,) + array.shape[1:])


def local(tokens, cotangent, expert_ids, gate_values, up_weight, down_weight):
    owners = lax.axis_size("ep")
    experts = owners // 2
    tok_rows, width = tokens.shape
    capacity = 5 * tok_rows // (2 * experts)
    assignments = 2 * tok_rows
    flat_ids = expert_ids.reshape(-1)
    onehot = (flat_ids[:, None] == jnp.arange(experts, dtype=jnp.int32)[None, :]).astype(jnp.int32)
    running_rank = jnp.cumsum(onehot, axis=0)
    slot_index = jnp.sum(onehot * running_rank, axis=1) - 1
    position = flat_ids * capacity + slot_index
    where_from = (
        jnp.full((experts * capacity,), -1, jnp.int32)
        .at[position]
        .set(jnp.arange(assignments, dtype=jnp.int32))
    )
    is_valid = where_from >= 0
    assign = jnp.where(is_valid, where_from, 0)
    token_index = assign // 2
    send_x = jnp.where(is_valid[:, None], tokens[token_index], jnp.zeros((), tokens.dtype)).reshape(
        experts, capacity, width
    )
    send_dy = jnp.where(
        is_valid[:, None], cotangent[token_index], jnp.zeros((), cotangent.dtype)
    ).reshape(experts, capacity, width)
    send_gate = jnp.where(is_valid, gate_values.reshape(-1)[assign], 0.0).reshape(experts, capacity)
    arrived = (
        lax.all_to_all(duplicate(send_x, owners), "ep", split_axis=0, concat_axis=0, tiled=True),
        lax.all_to_all(duplicate(send_dy, owners), "ep", split_axis=0, concat_axis=0, tiled=True),
        lax.all_to_all(
            duplicate(send_gate, owners).astype(jnp.bfloat16),
            "ep",
            split_axis=0,
            concat_axis=0,
            tiled=True,
        ).astype(jnp.float32),
    )
    token_part, gate_part, down_sum = expert_terms(
        arrived[0].reshape(-1, width),
        arrived[1].reshape(-1, width),
        arrived[2].reshape(-1),
        up_weight,
        down_weight,
    )
    returned_rows = (
        lax.all_to_all(
            token_part.reshape(owners, capacity, width),
            "ep",
            split_axis=0,
            concat_axis=0,
            tiled=True,
        ),
        lax.all_to_all(
            gate_part.reshape(owners, capacity).astype(jnp.bfloat16),
            "ep",
            split_axis=0,
            concat_axis=0,
            tiled=True,
        ).astype(jnp.float32),
    )
    token_terms = jnp.sum(
        returned_rows[0].reshape(experts, 2, capacity, width).astype(jnp.float32), axis=1
    ).reshape(experts * capacity, width)
    gate_terms = jnp.sum(returned_rows[1].reshape(experts, 2, capacity), axis=1).reshape(-1)
    token_grad = jnp.sum(token_terms[position].reshape(tok_rows, 2, width), axis=1).astype(
        jnp.bfloat16
    )
    gate_grad = gate_terms[position].reshape(tok_rows, 2)
    return (token_grad, gate_grad, down_sum)


def solution(mesh):
    return jax.shard_map(
        local,
        mesh=mesh,
        in_specs=(
            P(("ep", "rep"), None),
            P(("ep", "rep"), None),
            P(("ep", "rep"), None),
            P(("ep", "rep"), None),
            P("rep", "ep"),
            P("ep", "rep"),
        ),
        out_specs=(P(("ep", "rep"), None), P(("ep", "rep"), None), P("ep", "rep")),
        check_vma=False,
    )
```

profile of v0, /device:TPU:24, one launch (start us, length us, event | category | flops | bytes accessed | tf_op | source)
XLA Modules:
  0.0 719.4 jit_solution(11927677909159664940)
XLA Ops:
  10.2 1.4 scatter_custom_fusion
  12.6 2.4 gather_fusion
  15.9 19.8 %all-to-all-start = ((bf16[128,1,5]{2,1,0:T(2,128)(2,1)}), bf16[128,1,5]{2,1,0:T(2,128)(2,1)S(1)}, u32[]{:S(2)}, u32[]{:S(2)}) async-start(bf16[128,1,5]{2,1,0:T(2,128)(2,1)} %copy.27), calls=%async_computation | async-start | bytes 131072 | tf_op jit(solution)/shard_map/all_to_all | solution.py:87
  35.9 2.4 gather_fusion.1
  38.3 1.6 gather.21
  39.9 2.4 gather_fusion.2
  42.3 1.6 gather.23
  43.9 3.9 broadcast_select_fusion.1
  47.9 2.3 all-to-all-done
  50.2 2.1 broadcast_in_dim.64
  52.3 200.6 %all_to_all.27 = bf16[128,5,2048]{2,1,0:T(8,128)(2,1)} all-to-all(bf16[128,5,2048]{2,1,0:T(8,128)(2,1)S(1)} %bitcast.30), channel_id=1, replica_groups=mesh['ep'=128,'rep'=4] {'ep'}, dimensions={0} | all-to-all | bytes 5242880 | tf_op jit(solution)/shard_map/all_to_all | solution.py:85
  252.9 2.5 broadcast_in_dim.63
  255.4 10.6 %all-to-all-start.1 = ((bf16[128,5,2048]{2,1,0:T(8,128)(2,1)}), bf16[128,5,2048]{2,1,0:T(8,128)(2,1)}, u32[]{:S(2)}, u32[]{:S(2)}) async-start(bf16[128,5,2048]{2,1,0:T(8,128)(2,1)} %bitcast.29), calls=%async_computation.1 | async-start | bytes 8388608 | tf_op jit(solution)/shard_map/all_to_all | solution.py:86
  267.9 5.6 reshape.160
  273.5 179.0 %all-to-all-done.1 = bf16[128,5,2048]{2,1,0:T(8,128)(2,1)} async-done(((bf16[128,5,2048]{2,1,0:T(8,128)(2,1)}), bf16[128,5,2048]{2,1,0:T(8,128)(2,1)}, u32[]{:S(2)}, u32[]{:S(2)}) %all-to-all-start.1) | async-done | bytes 2621472 | tf_op jit(solution)/shard_map/all_to_all | solution.py:86
  452.4 4.2 reshape.158
  456.7 5.9 fusion.32
  462.6 5.7 multiply_reduce_fusion
  468.3 0.9 convert_element_type.107
  469.2 10.1 %all-to-all-start.4 = ((bf16[128,1,5]{2,1,0:T(2,128)(2,1)}), bf16[128,1,5]{2,1,0:T(2,128)(2,1)S(1)}, u32[]{:S(2)}, u32[]{:S(2)}) async-start(bf16[128,1,5]{2,1,0:T(2,128)(2,1)} %convert_element_type.107), calls=%async_computation.4 | async-start | bytes 131072 | tf_op jit(solution)/shard_map/all_to_all | solution.py:110
  479.3 7.3 %convolution_convert_fusion.1 = bf16[640,2048]{1,0:T(8,128)(2,1)} fusion(bf16[2048,640]{1,0:T(8,128)(2,1)} %all-gather.5.cloned.1.call-done, f32[640,640]{0,1:T(8,128)} %fusion.32, f32[640,640]{0,1:T(8,128)} %get-tuple-element.17, f32[640]{0:T(1024)S(1)} %reshape.166), kind=kOutput, calls=%fused_computation.9 | convolution fusion | flops 1687224320 | bytes 8522240 | tf_op jit(solution)/shard_map/dot_general | solution.py:47
  486.6 5.5 reshape.161
  492.1 1.7 all-to-all-done.4
  493.8 14.9 %all-to-all-start.3 = ((bf16[128,5,2048]{2,1,0:T(8,128)(2,1)}), bf16[128,5,2048]{2,1,0:T(8,128)(2,1)}, u32[]{:S(2)}, u32[]{:S(2)}) async-start(bf16[128,5,2048]{2,1,0:T(8,128)(2,1)} %reshape.161), calls=%async_computation.3 | async-start | bytes 8388608 | tf_op jit(solution)/shard_map/all_to_all | solution.py:103
  508.8 5.5 convolution_convert_fusion
  514.6 1.9 gather_fusion.4
  517.3 177.8 %all-to-all-done.3 = bf16[128,5,2048]{2,1,0:T(8,128)(2,1)} async-done(((bf16[128,5,2048]{2,1,0:T(8,128)(2,1)}), bf16[128,5,2048]{2,1,0:T(8,128)(2,1)}, u32[]{:S(2)}, u32[]{:S(2)}) %all-to-all-start.3) | async-done | bytes 2621472 | tf_op jit(solution)/shard_map/all_to_all | solution.py:103
  695.2 5.6 convert_reduce_fusion
  700.8 3.0 reshape.162
  703.8 2.7 gather_fusion.3
  706.5 2.5 reshape.163
  709.1 3.8 reduce_sum.47
  (49 shorter events, 8.0 us)
Async XLA Ops:
  7.2 28.7 %copy-start = (bf16[128,2048]{1,0:T(8,128)(2,1)S(1)}, bf16[128,2048]{1,0:T(8,128)(2,1)}, u32[]{:S(2)}) copy-start(bf16[128,2048]{1,0:T(8,128)(2,1)} %param.7) | copy-start | bytes 1572868
  15.9 34.3 %all-to-all-start = ((bf16[128,1,5]{2,1,0:T(2,128)(2,1)}), bf16[128,1,5]{2,1,0:T(2,128)(2,1)S(1)}, u32[]{:S(2)}, u32[]{:S(2)}) async-start(bf16[128,1,5]{2,1,0:T(2,128)(2,1)} %copy.27), calls=%async_computation | async-start | bytes 131072 | tf_op jit(solution)/shard_map/all_to_all | solution.py:87
  38.3 1.6 copy-start.2
  255.4 197.1 %all-to-all-start.1 = ((bf16[128,5,2048]{2,1,0:T(8,128)(2,1)}), bf16[128,5,2048]{2,1,0:T(8,128)(2,1)}, u32[]{:S(2)}, u32[]{:S(2)}) async-start(bf16[128,5,2048]{2,1,0:T(8,128)(2,1)} %bitcast.29), calls=%async_computation.1 | async-start | bytes 8388608 | tf_op jit(solution)/shard_map/all_to_all | solution.py:86
  266.0 190.6 %all-gather.5.cloned.1.call-start = ((), (), s32[]{:S(2)}) async-start(), calls=%async_computation.7 | async-start | bytes 3276800 | tf_op jit(solution)/shard_map/all_gather | solution.py:26
  266.8 195.9 %all-gather.3.cloned.1.call-start = ((), (), s32[]{:S(2)}) async-start(), calls=%async_computation.6 | async-start | bytes 3276800 | tf_op jit(solution)/shard_map/all_gather | solution.py:30
  469.2 24.6 %all-to-all-start.4 = ((bf16[128,1,5]{2,1,0:T(2,128)(2,1)}), bf16[128,1,5]{2,1,0:T(2,128)(2,1)S(1)}, u32[]{:S(2)}, u32[]{:S(2)}) async-start(bf16[128,1,5]{2,1,0:T(2,128)(2,1)} %convert_element_type.107), calls=%async_computation.4 | async-start | bytes 131072 | tf_op jit(solution)/shard_map/all_to_all | solution.py:110
  493.8 201.4 %all-to-all-start.3 = ((bf16[128,5,2048]{2,1,0:T(8,128)(2,1)}), bf16[128,5,2048]{2,1,0:T(8,128)(2,1)}, u32[]{:S(2)}, u32[]{:S(2)}) async-start(bf16[128,5,2048]{2,1,0:T(8,128)(2,1)} %reshape.161), calls=%async_computation.3 | async-start | bytes 8388608 | tf_op jit(solution)/shard_map/all_to_all | solution.py:103
  508.7 204.1 %reduce-scatter.2.cloned.1.call-start = ((), (), s32[]{:S(2)}) async-start(), calls=%async_computation.8 | async-start | bytes 3276800 | tf_op jit(solution)/shard_map/reduce_scatter | solution.py:42
  706.5 6.3 copy-start.1
Sparse Core Ops, SparseCore 0:
  268.9 41.3 all-gather.4
  312.4 42.9 all-gather.2
  514.4 40.2 reduce-scatter.1
where the time goes:
time: 721 us; the launch traced here: 719 us
  waiting for transfers between devices  362 us (50%)
  blocking collectives  201 us (28%)
  starting transfers between devices  55.7 us (8%)
  local copies, waits for them, and re-layouts  47.4 us (7%)
  matrix products  24.4 us (3%)
  other arithmetic  15.2 us (2%)
  between operations  14 us (2%)
    all_to_all x1, blocking collectives, local(): lax.all_to_all(duplicate(send_x, owners), 'ep', split_axis=0, concat_axis...  201 us
    all_to_all x1, waiting for transfers between devices, local(): lax.all_to_all(duplicate(send_dy, owners), 'ep', split_axis=0, concat_axi...  179 us
    all_to_all x1, waiting for transfers between devices, local(): lax.all_to_all(token_part.reshape(owners, capacity, width), 'ep', split_a...  178 us
    all_to_all x1, starting transfers between devices, local(): lax.all_to_all(duplicate(send_gate, owners).astype(jnp.bfloat16), 'ep', s...  19.8 us
    all_to_all x1, starting transfers between devices, local(): lax.all_to_all(token_part.reshape(owners, capacity, width), 'ep', split_a...  14.9 us
  transfers between devices with their start and end apart: 7, of which 4 were waited for; matrix products, arithmetic and copies ran while one was open for 9% of the time, Pallas kernels for 0%

commit v1 on v0

v1 whole, which is shorter than its diff:
```python
import math

import jax
import jax.numpy as jnp
from jax import lax
from jax.sharding import Mesh
from jax.sharding import PartitionSpec as P

tanh_scale = math.sqrt(2.0 / math.pi)
cubic_coef = 0.044715
EXTRA = 128


def gelu_tanh(argument):
    inner_arg = tanh_scale * (argument + cubic_coef * argument * argument * argument)
    return 0.5 * argument * (1.0 + jnp.tanh(inner_arg))


def gelu_slope(argument):
    tanh_value = jnp.tanh(tanh_scale * (argument + cubic_coef * argument * argument * argument))
    return 0.5 * (1.0 + tanh_value) + 0.5 * argument * (
        1.0 - tanh_value * tanh_value
    ) * tanh_scale * (1.0 + 3.0 * cubic_coef * argument * argument)


def split_bf16(value):
    high = value.astype(jnp.bfloat16)
    low = (value - high.astype(jnp.float32)).astype(jnp.bfloat16)
    return high, low


def expert_terms(rows_x, rows_dy, rows_gate, up_weight, down_weight):
    contract_last = (((1,), (1,)), ((), ()))
    up_full = lax.all_gather(up_weight, "rep", axis=0, tiled=True)
    down_full = lax.all_gather(down_weight, "rep", axis=1, tiled=True)
    pre_act = jnp.dot(rows_x, up_full, preferred_element_type=jnp.float32)
    grad_hidden = lax.dot_general(
        rows_dy, down_full, contract_last, preferred_element_type=jnp.float32
    )
    hidden = gelu_tanh(pre_act)
    hidden_bf = hidden.astype(jnp.bfloat16)
    gate_part = jnp.sum(hidden * grad_hidden, axis=1)
    scaled_dy = (rows_gate[:, None] * rows_dy.astype(jnp.float32)).astype(jnp.bfloat16)
    down_term = lax.dot_general(
        hidden_bf, scaled_dy, (((0,), (0,)), ((), ())), preferred_element_type=jnp.float32
    ).astype(jnp.bfloat16)
    down_sum = (
        lax.psum_scatter(down_term, "rep", scatter_dimension=1, tiled=True)
        .astype(jnp.float32)
        .astype(jnp.bfloat16)
    )
    grad_pre = (rows_gate[:, None] * grad_hidden * gelu_slope(pre_act)).astype(jnp.bfloat16)
    token_part = lax.dot_general(
        grad_pre, up_full, contract_last, preferred_element_type=jnp.float32
    ).astype(jnp.bfloat16)
    return (token_part, gate_part, down_sum)


def local(tokens, cotangent, expert_ids, gate_values, up_weight, down_weight):
    experts = lax.axis_size("epc")
    cores = lax.axis_size("core")
    core = lax.axis_index("core")
    tok_rows, width = tokens.shape
    capacity = 5 * tok_rows // (2 * experts)
    assignments = 2 * tok_rows
    flat_ids = expert_ids.reshape(-1)
    onehot = (flat_ids[:, None] == jnp.arange(experts, dtype=jnp.int32)[None, :]).astype(jnp.int32)
    running_rank = jnp.cumsum(onehot, axis=0)
    slot_index = jnp.sum(onehot * running_rank, axis=1) - 1
    position = flat_ids * capacity + slot_index
    where_from = (
        jnp.full((experts * capacity,), -1, jnp.int32)
        .at[position]
        .set(jnp.arange(assignments, dtype=jnp.int32))
    )
    is_valid = where_from >= 0
    assign = jnp.where(is_valid, where_from, 0)
    token_index = assign // 2
    send_x = jnp.where(is_valid[:, None], tokens[token_index], jnp.zeros((), tokens.dtype))
    send_dy = jnp.where(is_valid[:, None], cotangent[token_index], jnp.zeros((), cotangent.dtype))
    send_gate = jnp.where(is_valid, gate_values.reshape(-1)[assign], 0.0)
    gate_high, gate_low = split_bf16(send_gate)
    lane = jnp.arange(EXTRA, dtype=jnp.int32)[None, :]
    extra = jnp.where(
        lane == 0, gate_high[:, None], jnp.where(lane == 1, gate_low[:, None], jnp.zeros((), jnp.bfloat16))
    )
    send = jnp.concatenate([send_x, send_dy, extra], axis=1).reshape(experts, capacity, -1)
    arrived = lax.all_to_all(send, "epc", split_axis=0, concat_axis=0, tiled=True)
    both = lax.all_gather(arrived, "core", axis=0, tiled=False)
    rows = both.reshape(cores * experts * capacity, -1)
    rows_gate = rows[:, 2 * width].astype(jnp.float32) + rows[:, 2 * width + 1].astype(jnp.float32)
    token_part, gate_part, down_sum = expert_terms(
        rows[:, :width], rows[:, width : 2 * width], rows_gate, up_weight, down_weight
    )
    part_high, part_low = split_bf16(gate_part)
    back_lane = jnp.arange(EXTRA, dtype=jnp.int32)[None, :]
    back_extra = jnp.where(
        back_lane == 2 * core,
        part_high[:, None],
        jnp.where(back_lane == 2 * core + 1, part_low[:, None], jnp.zeros((), jnp.bfloat16)),
    )
    back = jnp.concatenate([token_part, back_extra], axis=1).reshape(cores, experts * capacity, -1)
    summed = lax.psum_scatter(back, "core", scatter_dimension=0, tiled=False)
    returned = lax.all_to_all(
        summed.reshape(experts, capacity, -1), "epc", split_axis=0, concat_axis=0, tiled=True
    ).reshape(experts * capacity, -1)
    picked = returned[position].astype(jnp.float32)
    token_grad = jnp.sum(picked[:, :width].reshape(tok_rows, 2, width), axis=1).astype(jnp.bfloat16)
    gate_grad = (
        (picked[:, width] + picked[:, width + 1]) + (picked[:, width + 2] + picked[:, width + 3])
    ).reshape(tok_rows, 2)
    return (token_grad, gate_grad, down_sum)


def solution(mesh):
    ep_size = mesh.shape["ep"]
    split_mesh = Mesh(
        mesh.devices.reshape(ep_size // 2, 2, mesh.shape["rep"]), ("epc", "core", "rep")
    )
    ep = ("epc", "core")
    return jax.shard_map(
        local,
        mesh=split_mesh,
        in_specs=(
            P(ep + ("rep",), None),
            P(ep + ("rep",), None),
            P(ep + ("rep",), None),
            P(ep + ("rep",), None),
            P("rep", ep),
            P(ep, "rep"),
        ),
        out_specs=(P(ep + ("rep",), None), P(ep + ("rep",), None), P(ep, "rep")),
        check_vma=False,
    )
```

time: 721 us -> 536 us (0.74)
  waiting for transfers between devices: 362 us -> 205 us
  starting transfers between devices: 55.7 us -> 16.2 us
  blocking collectives: 201 us -> 216 us
    all_to_all x4 -> x1, waiting for transfers between devices: 361 us -> 100 us  [local(): lax.all_to_all(summed.reshape(experts, capacity, -1), 'epc', split_axis=0...]
    all_gather x1 -> x2, waiting for transfers between devices: 0.01 us -> 54.4 us  [the longest x1 40.3 us: expert_terms(): down_full = lax.all_gather(down_weight, 'rep', axis=1, tiled=True)]
    all_to_all x4 -> x1, starting transfers between devices: 55.4 us -> 15.8 us  [local(): lax.all_to_all(summed.reshape(experts, capacity, -1), 'epc', split_axis=0...]
    all_gather x1, waiting for transfers between devices: 0.02 us -> 25.4 us  [expert_terms(): up_full = lax.all_gather(up_weight, 'rep', axis=0, tiled=True)]
    reduce_scatter x0 -> x1, waiting for transfers between devices: none -> 23.5 us  [local(): summed = lax.psum_scatter(back, 'core', scatter_dimension=0, tiled=False)]
    all_to_all x1, blocking collectives: 201 us -> 216 us  [local(): lax.all_to_all(send, 'epc', split_axis=0, concat_axis=0, tiled=True)]
    all_gather x0 -> x1, local copies, waits for them, and re-layouts: none -> 8.91 us  [local(): both = lax.all_gather(arrived, 'core', axis=0, tiled=False)]
    reshape x8 -> x4, local copies, waits for them, and re-layouts: 21.2 us -> 14.1 us  [the longest x1 8.82 us: local(): rows = both.reshape(cores * experts * capacity, -1)]
  transfers between devices with their start and end apart: 7 -> 6, of which waited for: 4 -> 5; matrix products, arithmetic and copies ran while one was open for 9% -> 8% of each run, Pallas kernels for 0% -> 0%
where the time goes in v1:
time: 536 us; the launch traced here: 535 us
  blocking collectives  216 us (40%)
  waiting for transfers between devices  205 us (38%)
  local copies, waits for them, and re-layouts  50.8 us (9%)
  matrix products  18.6 us (3%)
  starting transfers between devices  16.2 us (3%)
  other arithmetic  14.5 us (3%)
  between operations  14.1 us (3%)
    all_to_all x1, blocking collectives, local(): lax.all_to_all(send, 'epc', split_axis=0, concat_axis=0, tiled=True)  216 us
    all_to_all x1, waiting for transfers between devices, local(): lax.all_to_all(summed.reshape(experts, capacity, -1), 'epc', split_axis=0...  100 us
    all_gather x1, waiting for transfers between devices, expert_terms(): down_full = lax.all_gather(down_weight, 'rep', axis=1, tiled=True)  40.3 us
    all_gather x1, waiting for transfers between devices, expert_terms(): up_full = lax.all_gather(up_weight, 'rep', axis=0, tiled=True)  25.4 us
    reduce_scatter x1, waiting for transfers between devices, local(): summed = lax.psum_scatter(back, 'core', scatter_dimension=0, tiled=False)  23.5 us
    all_to_all x1, starting transfers between devices, local(): lax.all_to_all(summed.reshape(experts, capacity, -1), 'epc', split_axis=0...  15.8 us
    all_gather x1, waiting for transfers between devices, local(): both = lax.all_gather(arrived, 'core', axis=0, tiled=False)  14.1 us
  transfers between devices with their start and end apart: 6, of which 5 were waited for; matrix products, arithmetic and copies ran while one was open for 8% of the time, Pallas kernels for 0%

profile of v1, /device:TPU:24, one launch (start us, length us, event | category | flops | bytes accessed | tf_op | source)
XLA Modules:
  0.0 535.3 jit_solution(8706485857764557937)
XLA Ops:
  7.2 0.8 copy.17
  10.3 1.4 scatter_custom_fusion
  12.7 2.5 gather_fusion.2
  15.6 3.0 gather_fusion
  18.7 2.4 gather.17
  21.1 3.0 gather_fusion.1
  24.2 3.4 gather.19
  27.6 2.0 broadcast_select_fusion.1
  30.6 215.9 %all_to_all.10 = bf16[64,5,4224]{2,1,0:T(8,128)(2,1)S(1)} all-to-all(bf16[64,5,4224]{2,1,0:T(8,128)(2,1)S(1)} %pad_maximum_fusion), channel_id=1, replica_groups=mesh['epc'=64,'core'=2,'rep'=4] {'epc'}, dimensions={0} | all-to-all | bytes 5406720 | tf_op jit(solution)/shard_map/all_to_all | solution.py:88
  246.5 1.9 copy.21
  250.1 14.1 %all-gather.9.cloned.1.call-done = bf16[128,5,4224]{2,0,1:T(8,128)(2,1)} async-done(((bf16[64,5,4224]{2,0,1:T(8,128)(2,1)}), bf16[128,5,4224]{2,0,1:T(8,128)(2,1)}) %all-gather.9.cloned.1.call-update) | async-done | bytes 5406736 | tf_op jit(solution)/shard_map/all_gather | solution.py:89
  264.2 8.9 %copy.22 = bf16[128,5,4224]{2,1,0:T(8,128)(2,1)} copy(bf16[128,5,4224]{2,0,1:T(8,128)(2,1)} %all-gather.9.cloned.1.call-done) | data formatting | bytes 10813440 | tf_op jit(solution)/shard_map/all_gather | solution.py:89
  273.1 8.8 %reshape.148 = bf16[640,4224]{1,0:T(8,128)(2,1)} reshape(bf16[128,5,4224]{2,1,0:T(8,128)(2,1)} %copy.22) | data formatting | bytes 10813440 | tf_op jit(solution)/shard_map/reshape | solution.py:90
  281.9 1.2 add_reduce_fusion
  283.2 25.4 %all-gather.7.cloned.1.call-done = bf16[2048,640]{1,0:T(8,128)(2,1)} async-done(((bf16[512,640]{1,0:T(8,128)(2,1)}), bf16[2048,640]{1,0:T(8,128)(2,1)}) %all-gather.7.cloned.1.call-update) | async-done | bytes 2621456 | tf_op jit(solution)/shard_map/all_gather | solution.py:34
  308.6 4.8 fusion
  313.4 40.3 %all-gather.5.cloned.1.call-done = bf16[640,2048]{1,0:T(8,128)(2,1)} async-done(((bf16[640,512]{1,0:T(8,128)(2,1)}), bf16[640,2048]{1,0:T(8,128)(2,1)}) %all-gather.5.cloned.1.call-update) | async-done | bytes 2621456 | tf_op jit(solution)/shard_map/all_gather | solution.py:35
  353.7 5.1 multiply_reduce_fusion
  359.1 3.1 convolution_convert_fusion.1
  362.2 1.8 pad_maximum_fusion.1
  364.0 23.5 %reduce-scatter.3.cloned.1.call-done = bf16[1,320,2176]{2,1,0:T(8,128)(2,1)} async-done(((bf16[2,320,2176]{2,1,0:T(8,128)(2,1)}), bf16[1,320,2176]{2,1,0:T(8,128)(2,1)}) %reduce-scatter.3.cloned.1.call-update) | async-done | bytes 1392656 | tf_op jit(solution)/shard_map/reduce_scatter | solution.py:103
  387.5 3.5 reshape_reduce_scatter.3
  391.0 15.8 %all-to-all-start.1 = ((bf16[64,5,2176]{2,1,0:T(8,128)(2,1)}), bf16[64,5,2176]{2,1,0:T(8,128)(2,1)}, u32[]{:S(2)}, u32[]{:S(2)}) async-start(bf16[64,5,2176]{2,1,0:T(8,128)(2,1)} %reshape_reduce_scatter.3), calls=%async_computation.2 | async-start | bytes 4456448 | tf_op jit(solution)/shard_map/all_to_all | solution.py:104
  406.9 5.7 %convolution_convert_fusion = bf16[640,2048]{1,0:T(8,128)(2,1)} fusion(f32[640]{0:T(1024)S(1)} %add_reduce_fusion, bf16[640,4224]{1,0:T(8,128)(2,1)} %reshape.148, f32[640,640]{0,1:T(8,128)S(1)} %fusion), kind=kOutput, calls=%fused_computation.7 | convolution fusion | flops 1686650880 | bytes 6883840 | tf_op jit(solution)/shard_map/dot_general | solution.py:44
  412.6 100.3 %all-to-all-done.1 = bf16[64,5,2176]{2,1,0:T(8,128)(2,1)} async-done(((bf16[64,5,2176]{2,1,0:T(8,128)(2,1)}), bf16[64,5,2176]{2,1,0:T(8,128)(2,1)}, u32[]{:S(2)}, u32[]{:S(2)}) %all-to-all-start.1) | async-done | bytes 1392672 | tf_op jit(solution)/shard_map/all_to_all | solution.py:104
  512.9 2.6 reshape.150
  515.5 1.5 gather_fusion.3
  517.0 1.6 slice.57
  518.6 1.5 convert_element_type.83
  520.2 2.5 reshape.151
  522.7 1.5 fusion.22
  525.0 3.8 reduce_sum.29
  (53 shorter events, 7.4 us)
Async XLA Ops:
  7.2 8.5 %copy-start = (bf16[128,2048]{1,0:T(8,128)(2,1)S(1)}, bf16[128,2048]{1,0:T(8,128)(2,1)}, u32[]{:S(2)}) copy-start(bf16[128,2048]{1,0:T(8,128)(2,1)} %param.6) | copy-start | bytes 1572868
  7.2 257.0 %all-gather.9.cloned.1.call-start = ((), (), s32[]{:S(2)}) async-start(), calls=%async_computation.8 | async-start | bytes 8110080 | tf_op jit(solution)/shard_map/all_gather | solution.py:89
  18.7 2.4 copy-start.2
  248.4 60.2 %all-gather.7.cloned.1.call-start = ((), (), s32[]{:S(2)}) async-start(), calls=%async_computation.5 | async-start | bytes 3276800 | tf_op jit(solution)/shard_map/all_gather | solution.py:34
  249.1 104.6 %all-gather.5.cloned.1.call-start = ((), (), s32[]{:S(2)}) async-start(), calls=%async_computation.4 | async-start | bytes 3276800 | tf_op jit(solution)/shard_map/all_gather | solution.py:35
  249.9 137.6 %reduce-scatter.3.cloned.1.call-start = ((), (), s32[]{:S(2)}) async-start(), calls=%async_computation.6 | async-start | bytes 4177920 | tf_op jit(solution)/shard_map/reduce_scatter | solution.py:103
  353.7 5.3 copy-start.3
  391.0 121.9 %all-to-all-start.1 = ((bf16[64,5,2176]{2,1,0:T(8,128)(2,1)}), bf16[64,5,2176]{2,1,0:T(8,128)(2,1)}, u32[]{:S(2)}, u32[]{:S(2)}) async-start(bf16[64,5,2176]{2,1,0:T(8,128)(2,1)} %reshape_reduce_scatter.3), calls=%async_computation.2 | async-start | bytes 4456448 | tf_op jit(solution)/shard_map/all_to_all | solution.py:104
  406.8 121.9 %reduce-scatter.5.cloned.1.call-start = ((), (), s32[]{:S(2)}) async-start(), calls=%async_computation.7 | async-start | bytes 3276800 | tf_op jit(solution)/shard_map/reduce_scatter | solution.py:48
  520.2 8.6 %copy-start.1 = (bf16[128,2048]{1,0:T(8,128)(2,1)S(1)}, bf16[128,2048]{1,0:T(8,128)(2,1)}, u32[]{:S(2)}) copy-start(bf16[128,2048]{1,0:T(8,128)(2,1)} %param.6) | copy-start | bytes 1572868
Sparse Core Ops, SparseCore 0:
  248.5 15.6 all-gather.8
  266.3 42.2 all-gather.6
  310.7 42.9 all-gather.4
  364.1 23.3 reduce-scatter.2
  412.7 40.5 reduce-scatter.4

commit v2 on v1

--- a/solution.py
+++ b/solution.py
@@ -9,6 +9,7 @@
 tanh_scale = math.sqrt(2.0 / math.pi)
 cubic_coef = 0.044715
 EXTRA = 128
+LANES = 128
 
 
 def gelu_tanh(argument):
@@ -58,8 +59,6 @@
 
 def local(tokens, cotangent, expert_ids, gate_values, up_weight, down_weight):
     experts = lax.axis_size("epc")
-    cores = lax.axis_size("core")
-    core = lax.axis_index("core")
     tok_rows, width = tokens.shape
     capacity = 5 * tok_rows // (2 * experts)
     assignments = 2 * tok_rows
@@ -84,31 +83,57 @@
     extra = jnp.where(
         lane == 0, gate_high[:, None], jnp.where(lane == 1, gate_low[:, None], jnp.zeros((), jnp.bfloat16))
     )
-    send = jnp.concatenate([send_x, send_dy, extra], axis=1).reshape(experts, capacity, -1)
-    arrived = lax.all_to_all(send, "epc", split_axis=0, concat_axis=0, tiled=True)
-    both = lax.all_gather(arrived, "core", axis=0, tiled=False)
-    rows = both.reshape(cores * experts * capacity, -1)
+    send = jnp.concatenate([send_x, send_dy, extra], axis=1)
+    row_width = send.shape[1]
+    arrived = lax.all_to_all(
+        send.reshape(experts, capacity * row_width // LANES, LANES),
+        "epc",
+        split_axis=0,
+        concat_axis=0,
+        tiled=True,
+    ).reshape(experts * capacity, row_width)
+    swap = [(0, 1), (1, 0)]
+    partner_rows = lax.ppermute(arrived, "core", swap)
+    rows = jnp.concatenate([arrived, partner_rows], axis=0)
     rows_gate = rows[:, 2 * width].astype(jnp.float32) + rows[:, 2 * width + 1].astype(jnp.float32)
     token_part, gate_part, down_sum = expert_terms(
         rows[:, :width], rows[:, width : 2 * width], rows_gate, up_weight, down_weight
     )
-    part_high, part_low = split_bf16(gate_part)
+    own = experts * capacity
+    part_high, part_low = split_bf16(gate_part[own:])
     back_lane = jnp.arange(EXTRA, dtype=jnp.int32)[None, :]
     back_extra = jnp.where(
-        back_lane == 2 * core,
+        back_lane == 0,
         part_high[:, None],
-        jnp.where(back_lane == 2 * core + 1, part_low[:, None], jnp.zeros((), jnp.bfloat16)),
+        jnp.where(back_lane == 1, part_low[:, None], jnp.zeros((), jnp.bfloat16)),
     )
-    back = jnp.concatenate([token_part, back_extra], axis=1).reshape(cores, experts * capacity, -1)
-    summed = lax.psum_scatter(back, "core", scatter_dimension=0, tiled=False)
+    partner_back = lax.ppermute(
+        jnp.concatenate([token_part[own:], back_extra], axis=1), "core", swap
+    )
+    token_sum = (
+        token_part[:own].astype(jnp.float32) + partner_back[:, :width].astype(jnp.float32)
+    ).astype(jnp.bfloat16)
+    gate_sum = gate_part[:own] + (
+        partner_back[:, width].astype(jnp.float32) + partner_back[:, width + 1].astype(jnp.float32)
+    )
+    sum_high, sum_low = split_bf16(gate_sum)
+    ret_extra = jnp.where(
+        back_lane == 0,
+        sum_high[:, None],
+        jnp.where(back_lane == 1, sum_low[:, None], jnp.zeros((), jnp.bfloat16)),
+    )
+    back = jnp.concatenate([token_sum, ret_extra], axis=1)
+    back_width = back.shape[1]
     returned = lax.all_to_all(
-        summed.reshape(experts, capacity, -1), "epc", split_axis=0, concat_axis=0, tiled=True
-    ).reshape(experts * capacity, -1)
+        back.reshape(experts, capacity * back_width // LANES, LANES),
+        "epc",
+        split_axis=0,
+        concat_axis=0,
+        tiled=True,
+    ).reshape(experts * capacity, back_width)
     picked = returned[position].astype(jnp.float32)
     token_grad = jnp.sum(picked[:, :width].reshape(tok_rows, 2, width), axis=1).astype(jnp.bfloat16)
-    gate_grad = (
-        (picked[:, width] + picked[:, width + 1]) + (picked[:, width + 2] + picked[:, width + 3])
-    ).reshape(tok_rows, 2)
+    gate_grad = (picked[:, width] + picked[:, width + 1]).reshape(tok_rows, 2)
     return (token_grad, gate_grad, down_sum)
 
 

time: 536 us -> 343 us (0.64)
  blocking collectives: 216 us -> 0 us
  starting transfers between devices: 16.2 us -> 38.8 us
  local copies, waits for them, and re-layouts: 50.8 us -> 36.6 us
  waiting for transfers between devices: 205 us -> 219 us
    all_to_all x1 -> x0, blocking collectives: 216 us -> none  [local(): lax.all_to_all(send, 'epc', split_axis=0, concat_axis=0, tiled=True)]
    all_to_all x1 -> x2, waiting for transfers between devices: 100 us -> 193 us  [the longest x1 128 us: local(): lax.all_to_all(send.reshape(experts, capacity * row_width // LANES, LANES...]
    all_gather x1, waiting for transfers between devices: 25.4 us -> 0.02 us  [expert_terms(): up_full = lax.all_gather(up_weight, 'rep', axis=0, tiled=True)]
    reduce_scatter x1 -> x0, waiting for transfers between devices: 23.5 us -> none  [local(): summed = lax.psum_scatter(back, 'core', scatter_dimension=0, tiled=False)]
    all_gather x1, waiting for transfers between devices: 40.3 us -> 18.4 us  [expert_terms(): down_full = lax.all_gather(down_weight, 'rep', axis=1, tiled=True)]
    all_to_all x1 -> x2, starting transfers between devices: 15.8 us -> 34.4 us  [the longest x1 18.6 us: local(): lax.all_to_all(send.reshape(experts, capacity * row_width // LANES, LANES...]
    all_gather x1 -> x0, waiting for transfers between devices: 14.1 us -> none  [local(): both = lax.all_gather(arrived, 'core', axis=0, tiled=False)]
    all_gather x1 -> x0, local copies, waits for them, and re-layouts: 8.91 us -> none  [local(): both = lax.all_gather(arrived, 'core', axis=0, tiled=False)]
  transfers between devices with their start and end apart: 6 -> 7, of which waited for: 5 -> 5; matrix products, arithmetic and copies ran while one was open for 8% -> 10% of each run, Pallas kernels for 0% -> 0%
where the time goes in v2:
time: 343 us; the launch traced here: 341 us
  waiting for transfers between devices  219 us (64%)
  starting transfers between devices  38.8 us (11%)
  local copies, waits for them, and re-layouts  36.6 us (11%)
  matrix products  21.2 us (6%)
  between operations  14.1 us (4%)
  other arithmetic  11.3 us (3%)
    all_to_all x1, waiting for transfers between devices, local(): lax.all_to_all(send.reshape(experts, capacity * row_width // LANES, LANES...  128 us
    all_to_all x1, waiting for transfers between devices, local(): lax.all_to_all(back.reshape(experts, capacity * back_width // LANES, LANE...  65.8 us
    all_to_all x1, starting transfers between devices, local(): lax.all_to_all(send.reshape(experts, capacity * row_width // LANES, LANES...  18.6 us
    all_gather x1, waiting for transfers between devices, expert_terms(): down_full = lax.all_gather(down_weight, 'rep', axis=1, tiled=True)  18.4 us
    all_to_all x1, starting transfers between devices, local(): lax.all_to_all(back.reshape(experts, capacity * back_width // LANES, LANE...  15.9 us
  transfers between devices with their start and end apart: 7, of which 5 were waited for; matrix products, arithmetic and copies ran while one was open for 10% of the time, Pallas kernels for 0%

profile of v2, /device:TPU:24, one launch (start us, length us, event | category | flops | bytes accessed | tf_op | source)
XLA Modules:
  0.0 340.6 jit_solution(3544503409616689569)
XLA Ops:
  7.2 0.8 copy.11
  10.2 1.4 scatter_custom_fusion
  11.7 0.8 copy.14
  12.6 2.5 gather_fusion.2
  15.1 2.4 gather_fusion
  17.6 3.0 gather_fusion.1
  20.6 1.6 broadcast_select_fusion.1
  22.6 4.1 %reshape.101 = bf16[64,165,128]{2,1,0:T(8,128)(2,1)} reshape(bf16[320,4224]{1,0:T(8,128)(2,1)S(1)} %pad_maximum_fusion) | data formatting | bytes 5406720 | tf_op jit(solution)/shard_map/reshape | solution.py:89
  26.7 18.6 %all-to-all-start = ((bf16[64,165,128]{2,1,0:T(8,128)(2,1)}), bf16[64,165,128]{2,1,0:T(8,128)(2,1)S(1)}, u32[]{:S(2)}, u32[]{:S(2)}) async-start(bf16[64,165,128]{2,1,0:T(8,128)(2,1)} %reshape.101), calls=%async_computation | async-start | bytes 5505024 | tf_op jit(solution)/shard_map/all_to_all | solution.py:88
  46.1 127.5 %all-to-all-done = bf16[64,165,128]{2,1,0:T(8,128)(2,1)S(1)} async-done(((bf16[64,165,128]{2,1,0:T(8,128)(2,1)}), bf16[64,165,128]{2,1,0:T(8,128)(2,1)S(1)}, u32[]{:S(2)}, u32[]{:S(2)}) %all-to-all-start) | async-done | bytes 2703392 | tf_op jit(solution)/shard_map/all_to_all | solution.py:88
  173.6 3.9 %reshape.102 = bf16[320,4224]{1,0:T(8,128)(2,1)} reshape(bf16[64,165,128]{2,1,0:T(8,128)(2,1)S(1)} %all-to-all-done) | data formatting | bytes 5406720 | tf_op jit(solution)/shard_map/reshape | solution.py:94
  177.5 2.1 collective-permute-start
  179.7 1.9 constant_dynamic-update-slice_fusion.1
  181.6 3.0 collective-permute-done
  185.0 2.3 copy-done.2
  187.6 6.4 %fusion = f32[640,640]{0,1:T(8,128)} fusion(bf16[2048,640]{1,0:T(8,128)(2,1)} %all-gather.5.cloned.1.call-done, bf16[640,4224]{1,0:T(8,128)(2,1)} %copy-done.2), kind=kOutput, calls=%fused_computation.9 | convolution fusion | flops 1677721600 | bytes 6881280 | tf_op jit(solution)/shard_map/dot_general | solution.py:37
  194.0 18.4 %all-gather.3.cloned.1.call-done = bf16[640,2048]{1,0:T(8,128)(2,1)} async-done(((bf16[640,512]{1,0:T(8,128)(2,1)}), bf16[640,2048]{1,0:T(8,128)(2,1)}) %all-gather.3.cloned.1.call-update) | async-done | bytes 2621456 | tf_op jit(solution)/shard_map/all_gather | solution.py:36
  212.4 5.5 %multiply_reduce_fusion = (f32[640]{0:T(1024)S(1)}, f32[640,640]{0,1:T(8,128)S(1)}) fusion(f32[640,640]{0,1:T(8,128)} %fusion, bf16[640,2048]{1,0:T(8,128)(2,1)} %all-gather.3.cloned.1.call-done, bf16[640,4224]{1,0:T(8,128)(2,1)} %copy-done.2), kind=kOutput, calls=%fused_computation.25 | convolution fusion | flops 1681816960 | bytes 8522240 | tf_op jit(solution)/shard_map/dot_general | solution.py:38
  217.9 3.1 convolution_convert_fusion.1
  221.5 1.9 collective-permute-start.1
  223.5 3.1 collective-permute-done.1
  227.5 2.5 reshape.103
  230.0 15.9 %all-to-all-start.1 = ((bf16[64,85,128]{2,1,0:T(8,128)(2,1)}), bf16[64,85,128]{2,1,0:T(8,128)(2,1)}, u32[]{:S(2)}, u32[]{:S(2)}) async-start(bf16[64,85,128]{2,1,0:T(8,128)(2,1)} %reshape.103), calls=%async_computation.1 | async-start | bytes 2883584 | tf_op jit(solution)/shard_map/all_to_all | solution.py:127
  246.1 6.2 %convolution_convert_fusion = bf16[640,2048]{1,0:T(8,128)(2,1)} fusion(f32[640]{0:T(1024)S(1)} %add_reduce_fusion, bf16[640,4224]{1,0:T(8,128)(2,1)} %copy-done.2, f32[640,640]{0,1:T(8,128)} %fusion), kind=kOutput, calls=%fused_computation.6 | convolution fusion | flops 1686650880 | bytes 6883840 | tf_op jit(solution)/shard_map/dot_general | solution.py:45
  252.3 65.8 %all-to-all-done.1 = bf16[64,85,128]{2,1,0:T(8,128)(2,1)} async-done(((bf16[64,85,128]{2,1,0:T(8,128)(2,1)}), bf16[64,85,128]{2,1,0:T(8,128)(2,1)}, u32[]{:S(2)}, u32[]{:S(2)}) %all-to-all-start.1) | async-done | bytes 1392672 | tf_op jit(solution)/shard_map/all_to_all | solution.py:127
  318.2 3.1 reshape.104
  321.2 1.5 gather_fusion.3
  322.7 1.6 slice.82
  324.4 1.5 convert_element_type.102
  325.9 2.5 reshape.105
  328.4 1.2 fusion.21
  330.3 3.8 %reduce_sum.29 = bf16[128,2048]{1,0:T(8,128)(2,1)} reduce(f32[128,2,2048]{2,1,0:T(2,128)S(1)} %reshape.105, f32[]{:T(128)} %constant.22.clone.1), dimensions={1}, to_apply=%region_5.6 | reduce | flops 262144 | bytes 2621444 | tf_op jit(solution)/shard_map/reduce_sum | solution.py:135
  (54 shorter events, 6.6 us)
Async XLA Ops:
  7.2 8.0 %copy-start = (bf16[128,2048]{1,0:T(8,128)(2,1)S(1)}, bf16[128,2048]{1,0:T(8,128)(2,1)}, u32[]{:S(2)}) copy-start(bf16[128,2048]{1,0:T(8,128)(2,1)} %param.6) | copy-start | bytes 1572868
  15.1 2.5 copy-start.1
  26.7 146.9 %all-to-all-start = ((bf16[64,165,128]{2,1,0:T(8,128)(2,1)}), bf16[64,165,128]{2,1,0:T(8,128)(2,1)S(1)}, u32[]{:S(2)}, u32[]{:S(2)}) async-start(bf16[64,165,128]{2,1,0:T(8,128)(2,1)} %reshape.101), calls=%async_computation | async-start | bytes 5505024 | tf_op jit(solution)/shard_map/all_to_all | solution.py:88
  45.3 142.3 %all-gather.5.cloned.1.call-start = ((), (), s32[]{:S(2)}) async-start(), calls=%async_computation.4 | async-start | bytes 3276800 | tf_op jit(solution)/shard_map/all_gather | solution.py:35
  46.0 166.3 %all-gather.3.cloned.1.call-start = ((), (), s32[]{:S(2)}) async-start(), calls=%async_computation.3 | async-start | bytes 3276800 | tf_op jit(solution)/shard_map/all_gather | solution.py:36
  177.5 7.1 %collective-permute-start = (bf16[320,4224]{1,0:T(8,128)(2,1)}, bf16[320,4224]{1,0:T(8,128)(2,1)S(1)}, u32[]{:S(2)}, u32[]{:S(2)}) collective-permute-start(bf16[320,4224]{1,0:T(8,128)(2,1)} %reshape.102), channel_id=1, source_target_pairs={{0,4},{4,0},{1,5},{5,1},{2,6},{6,2},{3,7},{7,3},{8,12},{12,8},{9,1... | collective-permute-start | bytes 8110088 | tf_op jit(solution)/shard_map/ppermute | solution.py:96
  185.0 2.3 copy-start.2
  212.4 5.6 %copy-start.3 = (bf16[2048,640]{1,0:T(8,128)(2,1)S(1)}, bf16[2048,640]{1,0:T(8,128)(2,1)}, u32[]{:S(2)}) copy-start(bf16[2048,640]{1,0:T(8,128)(2,1)} %all-gather.5.cloned.1.call-done) | copy-start | bytes 7864324
  212.4 5.6 %copy-start.4 = (f32[640,640]{0,1:T(8,128)S(1)}, f32[640,640]{0,1:T(8,128)}, u32[]{:S(2)}) copy-start(f32[640,640]{0,1:T(8,128)} %fusion) | copy-start | bytes 4915204
  221.5 5.0 %collective-permute-start.1 = (bf16[320,2176]{1,0:T(8,128)(2,1)S(1)}, bf16[320,2176]{1,0:T(8,128)(2,1)S(1)}, u32[]{:S(2)}, u32[]{:S(2)}) collective-permute-start(bf16[320,2176]{1,0:T(8,128)(2,1)S(1)} %pad_maximum_fusion.1), channel_id=1, source_target_pairs={{0,4},{4,0},{1,5},{5,1},{2,6},{6,2},{3,7},{7,3},{8,12},{12,8},{9,1... | collective-permute-start | bytes 4177928 | tf_op jit(solution)/shard_map/ppermute | solution.py:110
  230.0 88.2 %all-to-all-start.1 = ((bf16[64,85,128]{2,1,0:T(8,128)(2,1)}), bf16[64,85,128]{2,1,0:T(8,128)(2,1)}, u32[]{:S(2)}, u32[]{:S(2)}) async-start(bf16[64,85,128]{2,1,0:T(8,128)(2,1)} %reshape.103), calls=%async_computation.1 | async-start | bytes 2883584 | tf_op jit(solution)/shard_map/all_to_all | solution.py:127
  245.8 88.2 %reduce-scatter.2.cloned.1.call-start = ((), (), s32[]{:S(2)}) async-start(), calls=%async_computation.5 | async-start | bytes 3276800 | tf_op jit(solution)/shard_map/reduce_scatter | solution.py:49
Sparse Core Ops, SparseCore 0:
  48.2 41.6 all-gather.4
  179.8 32.5 all-gather.2
  252.4 41.2 reduce-scatter.1

commit v3 on v2

--- a/solution.py
+++ b/solution.py
@@ -32,12 +32,12 @@
 
 def expert_terms(rows_x, rows_dy, rows_gate, up_weight, down_weight):
     contract_last = (((1,), (1,)), ((), ()))
-    up_full = lax.all_gather(up_weight, "rep", axis=0, tiled=True)
-    down_full = lax.all_gather(down_weight, "rep", axis=1, tiled=True)
+    both_full = lax.all_gather(
+        jnp.stack([up_weight, down_weight.T]), "rep", axis=1, tiled=True
+    )
+    up_full = both_full[0]
     pre_act = jnp.dot(rows_x, up_full, preferred_element_type=jnp.float32)
-    grad_hidden = lax.dot_general(
-        rows_dy, down_full, contract_last, preferred_element_type=jnp.float32
-    )
+    grad_hidden = jnp.dot(rows_dy, both_full[1], preferred_element_type=jnp.float32)
     hidden = gelu_tanh(pre_act)
     hidden_bf = hidden.astype(jnp.bfloat16)
     gate_part = jnp.sum(hidden * grad_hidden, axis=1)

time: 343 us -> 309 us (0.901)
  waiting for transfers between devices: 219 us -> 196 us
  starting transfers between devices: 38.8 us -> 29.1 us
  matrix products: 21.2 us -> 16.4 us
    all_gather x2 -> x1, waiting for transfers between devices: 18.4 us -> 0.02 us  [expert_terms(): lax.all_gather(jnp.stack([up_weight, down_weight.T]), 'rep', axis=1, tile...]
    all_to_all x1, starting transfers between devices: 15.9 us -> 6.06 us  [local(): lax.all_to_all(back.reshape(experts, capacity * back_width // LANES, LANE...]
    all_to_all x1, waiting for transfers between devices: 128 us -> 124 us  [local(): lax.all_to_all(send.reshape(experts, capacity * row_width // LANES, LANES...]
    unnamed x14 -> x17, local copies, waits for them, and re-layouts: 6.55 us -> 9.46 us
  transfers between devices with their start and end apart: 7 -> 6, of which waited for: 5 -> 4; matrix products, arithmetic and copies ran while one was open for 10% -> 11% of each run, Pallas kernels for 0% -> 0%
where the time goes in v3:
time: 309 us
  waiting for transfers between devices  196 us (63%)
  local copies, waits for them, and re-layouts  39.5 us (13%)
  starting transfers between devices  29.1 us (9%)
  matrix products  16.4 us (5%)
  between operations  14.4 us (5%)
  other arithmetic  13.8 us (4%)
    all_to_all x1, waiting for transfers between devices, local(): lax.all_to_all(send.reshape(experts, capacity * row_width // LANES, LANES...  124 us
    all_to_all x1, waiting for transfers between devices, local(): lax.all_to_all(back.reshape(experts, capacity * back_width // LANES, LANE...  65.9 us
    all_to_all x1, starting transfers between devices, local(): lax.all_to_all(send.reshape(experts, capacity * row_width // LANES, LANES...  18.6 us
    unnamed x17, local copies, waits for them, and re-layouts  9.46 us
  transfers between devices with their start and end apart: 6, of which 4 were waited for; matrix products, arithmetic and copies ran while one was open for 11% of the time, Pallas kernels for 0%

profile of v3, /device:TPU:24, one launch (start us, length us, event | category | flops | bytes accessed | tf_op | source)
XLA Modules:
  0.0 308.8 jit_solution(9349467961405495057)
XLA Ops:
  7.2 0.8 copy.12
  10.2 1.4 scatter_custom_fusion
  12.6 2.5 gather_fusion.2
  15.1 2.4 gather_fusion
  17.6 3.0 gather_fusion.1
  20.6 1.6 broadcast_select_fusion.1
  22.6 4.2 %reshape.101 = bf16[64,165,128]{2,1,0:T(8,128)(2,1)} reshape(bf16[320,4224]{1,0:T(8,128)(2,1)S(1)} %pad_maximum_fusion) | data formatting | bytes 5406720 | tf_op jit(solution)/shard_map/reshape | solution.py:89
  26.7 18.6 %all-to-all-start = ((bf16[64,165,128]{2,1,0:T(8,128)(2,1)}), bf16[64,165,128]{2,1,0:T(8,128)(2,1)S(1)}, u32[]{:S(2)}, u32[]{:S(2)}) async-start(bf16[64,165,128]{2,1,0:T(8,128)(2,1)} %reshape.101), calls=%async_computation | async-start | bytes 5505024 | tf_op jit(solution)/shard_map/all_to_all | solution.py:88
  45.3 2.2 copy.16
  47.5 2.5 pad_maximum_fusion.3
  50.0 123.6 %all-to-all-done = bf16[64,165,128]{2,1,0:T(8,128)(2,1)S(1)} async-done(((bf16[64,165,128]{2,1,0:T(8,128)(2,1)}), bf16[64,165,128]{2,1,0:T(8,128)(2,1)S(1)}, u32[]{:S(2)}, u32[]{:S(2)}) %all-to-all-start) | async-done | bytes 2703392 | tf_op jit(solution)/shard_map/all_to_all | solution.py:88
  173.6 4.0 %reshape.102 = bf16[320,4224]{1,0:T(8,128)(2,1)} reshape(bf16[64,165,128]{2,1,0:T(8,128)(2,1)S(1)} %all-to-all-done) | data formatting | bytes 5406720 | tf_op jit(solution)/shard_map/reshape | solution.py:94
  177.6 2.1 collective-permute-start
  179.7 1.9 constant_dynamic-update-slice_fusion.1
  181.6 3.1 collective-permute-done
  185.1 2.3 copy-done.2
  187.7 4.9 %fusion = f32[640,640]{0,1:T(8,128)S(1)} fusion(bf16[640,4224]{1,0:T(8,128)(2,1)} %copy-done.2, bf16[2,2048,640]{1,2,0:T(8,128)(2,1)} %all-gather.2.cloned.1.call-done), kind=kOutput, calls=%fused_computation.10 | convolution fusion | flops 1677721600 | bytes 6881280 | tf_op jit(solution)/shard_map/dot_general | solution.py:39
  193.3 2.4 multiply_reduce_fusion
  195.8 2.9 convolution_convert_fusion.1
  199.2 2.1 collective-permute-start.1
  201.3 3.0 collective-permute-done.1
  205.2 2.5 reshape.103
  207.7 6.1 %all-to-all-start.1 = ((bf16[64,85,128]{2,1,0:T(8,128)(2,1)}), bf16[64,85,128]{2,1,0:T(8,128)(2,1)}, u32[]{:S(2)}, u32[]{:S(2)}) async-start(bf16[64,85,128]{2,1,0:T(8,128)(2,1)} %reshape.103), calls=%async_computation.1 | async-start | bytes 2883584 | tf_op jit(solution)/shard_map/all_to_all | solution.py:127
  214.0 6.2 %convolution_convert_fusion = bf16[640,2048]{1,0:T(8,128)(2,1)} fusion(f32[640]{0:T(1024)S(1)} %add_reduce_fusion, bf16[640,4224]{1,0:T(8,128)(2,1)} %copy-done.2, f32[640,640]{0,1:T(8,128)} %copy-done.5), kind=kOutput, calls=%fused_computation.6 | convolution fusion | flops 1686650880 | bytes 6883840 | tf_op jit(solution)/shard_map/dot_general | solution.py:45
  220.2 65.9 %all-to-all-done.1 = bf16[64,85,128]{2,1,0:T(8,128)(2,1)} async-done(((bf16[64,85,128]{2,1,0:T(8,128)(2,1)}), bf16[64,85,128]{2,1,0:T(8,128)(2,1)}, u32[]{:S(2)}, u32[]{:S(2)}) %all-to-all-start.1) | async-done | bytes 1392672 | tf_op jit(solution)/shard_map/all_to_all | solution.py:127
  286.1 3.1 reshape.104
  289.1 1.5 gather_fusion.3
  290.6 1.6 slice.92
  292.2 1.5 convert_element_type.102
  293.7 2.5 reshape.105
  296.2 1.2 fusion.21
  298.2 3.8 %reduce_sum.29 = bf16[128,2048]{1,0:T(8,128)(2,1)} reduce(f32[128,2,2048]{2,1,0:T(2,128)S(1)} %reshape.105, f32[]{:T(128)} %constant.22.clone.1), dimensions={1}, to_apply=%region_5.6 | reduce | flops 262144 | bytes 2621444 | tf_op jit(solution)/shard_map/reduce_sum | solution.py:135
  (55 shorter events, 7.4 us)
Async XLA Ops:
  7.2 8.0 %copy-start = (bf16[128,2048]{1,0:T(8,128)(2,1)S(1)}, bf16[128,2048]{1,0:T(8,128)(2,1)}, u32[]{:S(2)}) copy-start(bf16[128,2048]{1,0:T(8,128)(2,1)} %param.6) | copy-start | bytes 1572868
  15.1 2.5 copy-start.1
  26.7 146.9 %all-to-all-start = ((bf16[64,165,128]{2,1,0:T(8,128)(2,1)}), bf16[64,165,128]{2,1,0:T(8,128)(2,1)S(1)}, u32[]{:S(2)}, u32[]{:S(2)}) async-start(bf16[64,165,128]{2,1,0:T(8,128)(2,1)} %reshape.101), calls=%async_computation | async-start | bytes 5505024 | tf_op jit(solution)/shard_map/all_to_all | solution.py:88
  45.3 142.4 %all-gather.2.cloned.1.call-start = ((), (), s32[]{:S(2)}) async-start(), calls=%async_computation.3 | async-start | bytes 6553600 | tf_op jit(solution)/shard_map/all_gather | solution.py:35
  177.6 7.1 %collective-permute-start = (bf16[320,4224]{1,0:T(8,128)(2,1)}, bf16[320,4224]{1,0:T(8,128)(2,1)S(1)}, u32[]{:S(2)}, u32[]{:S(2)}) collective-permute-start(bf16[320,4224]{1,0:T(8,128)(2,1)} %reshape.102), channel_id=1, source_target_pairs={{0,4},{4,0},{1,5},{5,1},{2,6},{6,2},{3,7},{7,3},{8,12},{12,8},{9,1... | collective-permute-start | bytes 8110088 | tf_op jit(solution)/shard_map/ppermute | solution.py:96
  185.0 2.3 copy-start.2
  187.7 4.9 %copy-start.3 = (bf16[640,4224]{1,0:T(8,128)(2,1)S(1)}, bf16[640,4224]{1,0:T(8,128)(2,1)}, u32[]{:S(2)}) copy-start(bf16[640,4224]{1,0:T(8,128)(2,1)} %copy-done.2) | copy-start | bytes 16220164
  187.7 5.7 %copy-start.4 = (bf16[2,2048,640]{1,2,0:T(8,128)(2,1)S(1)}, bf16[2,2048,640]{1,2,0:T(8,128)(2,1)}, u32[]{:S(2)}) copy-start(bf16[2,2048,640]{1,2,0:T(8,128)(2,1)} %all-gather.2.cloned.1.call-done) | copy-start | bytes 15728644
  193.3 2.4 copy-start.5
  199.2 5.0 %collective-permute-start.1 = (bf16[320,2176]{1,0:T(8,128)(2,1)S(1)}, bf16[320,2176]{1,0:T(8,128)(2,1)S(1)}, u32[]{:S(2)}, u32[]{:S(2)}) collective-permute-start(bf16[320,2176]{1,0:T(8,128)(2,1)S(1)} %pad_maximum_fusion.1), channel_id=1, source_target_pairs={{0,4},{4,0},{1,5},{5,1},{2,6},{6,2},{3,7},{7,3},{8,12},{12,8},{9,1... | collective-permute-start | bytes 4177928 | tf_op jit(solution)/shard_map/ppermute | solution.py:110
  207.7 78.4 %all-to-all-start.1 = ((bf16[64,85,128]{2,1,0:T(8,128)(2,1)}), bf16[64,85,128]{2,1,0:T(8,128)(2,1)}, u32[]{:S(2)}, u32[]{:S(2)}) async-start(bf16[64,85,128]{2,1,0:T(8,128)(2,1)} %reshape.103), calls=%async_computation.1 | async-start | bytes 2883584 | tf_op jit(solution)/shard_map/all_to_all | solution.py:127
  213.7 88.2 %reduce-scatter.2.cloned.1.call-start = ((), (), s32[]{:S(2)}) async-start(), calls=%async_computation.4 | async-start | bytes 3276800 | tf_op jit(solution)/shard_map/reduce_scatter | solution.py:49
Sparse Core Ops, SparseCore 0:
  50.1 63.6 all-gather.1
  220.3 40.4 reduce-scatter.1

commit v4 on v1

--- a/solution.py
+++ b/solution.py
@@ -8,7 +8,7 @@
 
 tanh_scale = math.sqrt(2.0 / math.pi)
 cubic_coef = 0.044715
-EXTRA = 128
+LANES = 128
 
 
 def gelu_tanh(argument):
@@ -31,12 +31,12 @@
 
 def expert_terms(rows_x, rows_dy, rows_gate, up_weight, down_weight):
     contract_last = (((1,), (1,)), ((), ()))
-    up_full = lax.all_gather(up_weight, "rep", axis=0, tiled=True)
-    down_full = lax.all_gather(down_weight, "rep", axis=1, tiled=True)
+    both_full = lax.all_gather(
+        jnp.stack([up_weight, down_weight.T]), "rep", axis=1, tiled=True
+    )
+    up_full = both_full[0]
     pre_act = jnp.dot(rows_x, up_full, preferred_element_type=jnp.float32)
-    grad_hidden = lax.dot_general(
-        rows_dy, down_full, contract_last, preferred_element_type=jnp.float32
-    )
+    grad_hidden = jnp.dot(rows_dy, both_full[1], preferred_element_type=jnp.float32)
     hidden = gelu_tanh(pre_act)
     hidden_bf = hidden.astype(jnp.bfloat16)
     gate_part = jnp.sum(hidden * grad_hidden, axis=1)
@@ -56,10 +56,36 @@
     return (token_part, gate_part, down_sum)
 
 
+def pack(rows, gate, experts):
+    count, row_width = rows.shape
+    per = count // experts
+    high, low = split_bf16(gate)
+    gate_row = jnp.concatenate(
+        [
+            high.reshape(experts, per),
+            low.reshape(experts, per),
+            jnp.zeros((experts, LANES - 2 * per), jnp.bfloat16),
+        ],
+        axis=1,
+    )
+    return jnp.concatenate(
+        [rows.reshape(experts, per * row_width // LANES, LANES), gate_row[:, None, :]], axis=1
+    )
+
+
+def unpack(packed, per):
+    experts = packed.shape[0]
+    body = packed[:, :-1].reshape(experts * per, -1)
+    gate_row = packed[:, -1].astype(jnp.float32)
+    return body, (gate_row[:, :per] + gate_row[:, per : 2 * per]).reshape(-1)
+
+
+def exchange(packed):
+    return lax.all_to_all(packed, "epc", split_axis=0, concat_axis=0, tiled=True)
+
+
 def local(tokens, cotangent, expert_ids, gate_values, up_weight, down_weight):
     experts = lax.axis_size("epc")
-    cores = lax.axis_size("core")
-    core = lax.axis_index("core")
     tok_rows, width = tokens.shape
     capacity = 5 * tok_rows // (2 * experts)
     assignments = 2 * tok_rows
@@ -79,36 +105,29 @@
     send_x = jnp.where(is_valid[:, None], tokens[token_index], jnp.zeros((), tokens.dtype))
     send_dy = jnp.where(is_valid[:, None], cotangent[token_index], jnp.zeros((), cotangent.dtype))
     send_gate = jnp.where(is_valid, gate_values.reshape(-1)[assign], 0.0)
-    gate_high, gate_low = split_bf16(send_gate)
-    lane = jnp.arange(EXTRA, dtype=jnp.int32)[None, :]
-    extra = jnp.where(
-        lane == 0, gate_high[:, None], jnp.where(lane == 1, gate_low[:, None], jnp.zeros((), jnp.bfloat16))
+    arrived = exchange(pack(jnp.concatenate([send_x, send_dy], axis=1), send_gate, experts))
+    swap = [(0, 1), (1, 0)]
+    own_rows, own_gate = unpack(arrived, capacity)
+    partner_rows, partner_gate = unpack(lax.ppermute(arrived, "core", swap), capacity)
+    rows = jnp.concatenate([own_rows, partner_rows], axis=0)
+    rows_gate = jnp.concatenate([own_gate, partner_gate], axis=0)
+    token_part, gate_part, down_sum = expert_terms(
+        rows[:, :width], rows[:, width:], rows_gate, up_weight, down_weight
     )
-    send = jnp.concatenate([send_x, send_dy, extra], axis=1).reshape(experts, capacity, -1)
-    arrived = lax.all_to_all(send, "epc", split_axis=0, concat_axis=0, tiled=True)
-    both = lax.all_gather(arrived, "core", axis=0, tiled=False)
-    rows = both.reshape(cores * experts * capacity, -1)
-    rows_gate = rows[:, 2 * width].astype(jnp.float32) + rows[:, 2 * width + 1].astype(jnp.float32)
-    token_part, gate_part, down_sum = expert_terms(
-        rows[:, :width], rows[:, width : 2 * width], rows_gate, up_weight, down_weight
+    own = experts * capacity
+    partner_token, partner_part = unpack(
+        lax.ppermute(pack(token_part[own:], gate_part[own:], experts), "core", swap), capacity
     )
-    part_high, part_low = split_bf16(gate_part)
-    back_lane = jnp.arange(EXTRA, dtype=jnp.int32)[None, :]
-    back_extra = jnp.where(
-        back_lane == 2 * core,
-        part_high[:, None],
-        jnp.where(back_lane == 2 * core + 1, part_low[:, None], jnp.zeros((), jnp.bfloat16)),
-    )
-    back = jnp.concatenate([token_part, back_extra], axis=1).reshape(cores, experts * capacity, -1)
-    summed = lax.psum_scatter(back, "core", scatter_dimension=0, tiled=False)
-    returned = lax.all_to_all(
-        summed.reshape(experts, capacity, -1), "epc", split_axis=0, concat_axis=0, tiled=True
-    ).reshape(experts * capacity, -1)
-    picked = returned[position].astype(jnp.float32)
-    token_grad = jnp.sum(picked[:, :width].reshape(tok_rows, 2, width), axis=1).astype(jnp.bfloat16)
-    gate_grad = (
-        (picked[:, width] + picked[:, width + 1]) + (picked[:, width + 2] + picked[:, width + 3])
-    ).reshape(tok_rows, 2)
+    token_sum = (
+        token_part[:own].astype(jnp.float32) + partner_token.astype(jnp.float32)
+    ).astype(jnp.bfloat16)
+    gate_sum = gate_part[:own] + partner_part
+    returned, returned_gate = unpack(exchange(pack(token_sum, gate_sum, experts)), capacity)
+    pair = position.reshape(tok_rows, 2)
+    token_grad = (
+        returned[pair[:, 0]].astype(jnp.float32) + returned[pair[:, 1]].astype(jnp.float32)
+    ).astype(jnp.bfloat16)
+    gate_grad = returned_gate[position].reshape(tok_rows, 2)
     return (token_grad, gate_grad, down_sum)
 
 

time: 536 us -> 330 us (0.62)
  blocking collectives: 216 us -> 0 us
  starting transfers between devices: 16.2 us -> 29.2 us
  waiting for transfers between devices: 205 us -> 192 us
  local copies, waits for them, and re-layouts: 50.8 us -> 58.4 us
    all_to_all x1 -> x0, blocking collectives: 216 us -> none  [local(): lax.all_to_all(send, 'epc', split_axis=0, concat_axis=0, tiled=True)]
    all_to_all x1 -> x2, waiting for transfers between devices: 100 us -> 190 us  [exchange(): lax.all_to_all(packed, 'epc', split_axis=0, concat_axis=0, tiled=True)]
    all_gather x3 -> x1, waiting for transfers between devices: 79.8 us -> 0.01 us  [expert_terms(): lax.all_gather(jnp.stack([up_weight, down_weight.T]), 'rep', axis=1, tile...]
    reduce_scatter x1 -> x0, waiting for transfers between devices: 23.5 us -> none  [local(): summed = lax.psum_scatter(back, 'core', scatter_dimension=0, tiled=False)]
    all_gather x1 -> x0, local copies, waits for them, and re-layouts: 8.91 us -> none  [local(): both = lax.all_gather(arrived, 'core', axis=0, tiled=False)]
    all_to_all x1 -> x2, starting transfers between devices: 15.8 us -> 24.4 us  [exchange(): lax.all_to_all(packed, 'epc', split_axis=0, concat_axis=0, tiled=True)]
    slice x2 -> x10, local copies, waits for them, and re-layouts: 1.82 us -> 9.01 us  [the longest x4 8.29 us: unpack(): body = packed[:, :-1].reshape(experts * per, -1)]
    unnamed x11 -> x19, local copies, waits for them, and re-layouts: 2.28 us -> 8.33 us
  transfers between devices with their start and end apart: 6 -> 6, of which waited for: 5 -> 3; matrix products, arithmetic and copies ran while one was open for 8% -> 13% of each run, Pallas kernels for 0% -> 0%
where the time goes in v4:
time: 330 us; the launch traced here: 329 us
  waiting for transfers between devices  192 us (58%)
  local copies, waits for them, and re-layouts  58.4 us (18%)
  starting transfers between devices  29.2 us (9%)
  matrix products  19.8 us (6%)
  other arithmetic  15.4 us (5%)
  between operations  14.5 us (4%)
    all_to_all x2, waiting for transfers between devices, exchange(): lax.all_to_all(packed, 'epc', split_axis=0, concat_axis=0, tiled=True)  190 us
    all_to_all x2, starting transfers between devices, exchange(): lax.all_to_all(packed, 'epc', split_axis=0, concat_axis=0, tiled=True)  24.4 us
    reshape x3, local copies, waits for them, and re-layouts, unpack(): body = packed[:, :-1].reshape(experts * per, -1)  10 us
    unnamed x19, local copies, waits for them, and re-layouts  8.33 us
    slice x4, local copies, waits for them, and re-layouts, unpack(): body = packed[:, :-1].reshape(experts * per, -1)  8.29 us
  transfers between devices with their start and end apart: 6, of which 3 were waited for; matrix products, arithmetic and copies ran while one was open for 13% of the time, Pallas kernels for 0%

profile of v4, /device:TPU:24, one launch (start us, length us, event | category | flops | bytes accessed | tf_op | source)
XLA Modules:
  0.0 329.5 jit_solution(13812891379042860833)
XLA Ops:
  12.0 2.5 gather_fusion.2
  15.0 2.4 gather_fusion.1
  17.5 3.0 gather_fusion
  22.2 3.1 reshape.139
  25.4 3.5 %pad_maximum_fusion = bf16[64,161,128]{2,1,0:T(8,128)(2,1)} fusion(bf16[64,1,128]{2,1,0:T(2,128)(2,1)S(1)} %copy.67, bf16[64,160,128]{2,1,0:T(8,128)(2,1)} %reshape.139), kind=kLoop, calls=%fused_computation.10 | loop fusion | flops 5275648 | bytes 5275648 | tf_op jit(solution)/shard_map/concatenate | solution.py:71
  28.8 18.6 %all-to-all-start = ((bf16[64,161,128]{2,1,0:T(8,128)(2,1)}), bf16[64,161,128]{2,1,0:T(8,128)(2,1)S(1)}, u32[]{:S(2)}, u32[]{:S(2)}) async-start(bf16[64,161,128]{2,1,0:T(8,128)(2,1)} %pad_maximum_fusion), calls=%async_computation | async-start | bytes 5505024 | tf_op jit(solution)/shard_map/all_to_all | solution.py:84
  47.5 2.2 copy.70
  49.6 2.5 pad_maximum_fusion.4
  52.1 123.6 %all-to-all-done = bf16[64,161,128]{2,1,0:T(8,128)(2,1)S(1)} async-done(((bf16[64,161,128]{2,1,0:T(8,128)(2,1)}), bf16[64,161,128]{2,1,0:T(8,128)(2,1)S(1)}, u32[]{:S(2)}, u32[]{:S(2)}) %all-to-all-start) | async-done | bytes 2637856 | tf_op jit(solution)/shard_map/all_to_all | solution.py:84
  175.7 2.2 copy.68
  177.9 2.1 collective-permute-start
  180.3 1.7 slice.157
  181.9 3.8 %reshape.145 = bf16[320,4096]{1,0:T(8,128)(2,1)S(1)} reshape(bf16[64,160,128]{2,1,0:T(8,128)(2,1)} %slice.157) | data formatting | bytes 5242880 | tf_op jit(solution)/shard_map/reshape | solution.py:78
  185.8 1.7 constant_dynamic-update-slice_fusion.1
  187.5 2.3 slice.158
  189.8 3.2 copy.69
  192.9 3.8 %reshape.146 = bf16[320,4096]{1,0:T(8,128)(2,1)S(1)} reshape(bf16[64,160,128]{2,1,0:T(8,128)(2,1)} %copy.69) | data formatting | bytes 5242880 | tf_op jit(solution)/shard_map/reshape | solution.py:78
  197.7 1.7 constant_dynamic-update-slice_fusion
  199.4 4.9 %fusion = f32[640,640]{0,1:T(8,128)S(1)} fusion(bf16[640,4096]{1,0:T(8,128)(2,1)} %constant_dynamic-update-slice_fusion, bf16[2,2048,640]{1,2,0:T(8,128)(2,1)} %all-gather.2.cloned.1.call-done), kind=kOutput, calls=%fused_computation.12 | convolution fusion | flops 1677721600 | bytes 6881280 | tf_op jit(solution)/shard_map/dot_general | solution.py:38
  205.0 3.6 %multiply_reduce_fusion = (f32[640]{0:T(1024)S(1)}, f32[640,640]{0,1:T(8,128)}) fusion(f32[640,640]{0,1:T(8,128)S(1)} %fusion, bf16[2,2048,640]{1,2,0:T(8,128)(2,1)S(1)} %copy-done.5, bf16[640,4096]{1,0:T(8,128)(2,1)S(1)} %copy-done.4), kind=kOutput, calls=%fused_computation.30 | convolution fusion | flops 1681816960 | bytes 8522240 | tf_op jit(solution)/shard_map/dot_general | solution.py:39
  209.2 5.1 %convolution_convert_fusion.1 = bf16[640,2048]{1,0:T(8,128)(2,1)S(1)} fusion(bf16[2,2048,640]{1,2,0:T(8,128)(2,1)} %all-gather.2.cloned.1.call-done, f32[640,640]{0,1:T(8,128)S(1)} %fusion, f32[640,640]{0,1:T(8,128)} %get-tuple-element.33, f32[640]{0:T(1024)S(1)} %pad_maximum_fusion.5), kind=kOutput, calls=%fused_computation.9 | convolution fusion | flops 1687224320 | bytes 8522240 | tf_op jit(solution)/shard_map/dot_general | solution.py:53
  217.2 2.6 collective-permute-start.1
  220.0 2.3 collective-permute-done.1
  222.8 3.0 copy.76
  225.8 2.6 reshape.154
  228.4 2.8 add_convert_fusion
  231.2 2.4 reshape.148
  234.8 5.8 %all-to-all-start.1 = ((bf16[64,81,128]{2,1,0:T(8,128)(2,1)}), bf16[64,81,128]{2,1,0:T(8,128)(2,1)S(1)}, u32[]{:S(2)}, u32[]{:S(2)}) async-start(bf16[64,81,128]{2,1,0:T(8,128)(2,1)} %pad_maximum_fusion.2), calls=%async_computation.1 | async-start | bytes 2883584 | tf_op jit(solution)/shard_map/all_to_all | solution.py:84
  240.7 6.2 %convolution_convert_fusion = bf16[640,2048]{1,0:T(8,128)(2,1)} fusion(f32[640]{0:T(1024)S(1)} %pad_maximum_fusion.5, bf16[640,4096]{1,0:T(8,128)(2,1)} %constant_dynamic-update-slice_fusion, f32[640,640]{0,1:T(8,128)} %copy-done.6), kind=kOutput, calls=%fused_computation.8 | convolution fusion | flops 1686650880 | bytes 6883840 | tf_op jit(solution)/shard_map/dot_general | solution.py:44
  247.1 66.2 %all-to-all-done.1 = bf16[64,81,128]{2,1,0:T(8,128)(2,1)S(1)} async-done(((bf16[64,81,128]{2,1,0:T(8,128)(2,1)}), bf16[64,81,128]{2,1,0:T(8,128)(2,1)S(1)}, u32[]{:S(2)}, u32[]{:S(2)}) %all-to-all-start.1) | async-done | bytes 1327136 | tf_op jit(solution)/shard_map/all_to_all | solution.py:84
  314.5 2.4 reshape.149
  317.1 1.9 gather_fusion.5
  (89 shorter events, 19.3 us)
Async XLA Ops:
  7.2 7.8 %copy-start = (bf16[128,2048]{1,0:T(8,128)(2,1)S(1)}, bf16[128,2048]{1,0:T(8,128)(2,1)}, u32[]{:S(2)}) copy-start(bf16[128,2048]{1,0:T(8,128)(2,1)} %param.7) | copy-start | bytes 1572868
  15.0 2.5 copy-start.2
  28.8 146.9 %all-to-all-start = ((bf16[64,161,128]{2,1,0:T(8,128)(2,1)}), bf16[64,161,128]{2,1,0:T(8,128)(2,1)S(1)}, u32[]{:S(2)}, u32[]{:S(2)}) async-start(bf16[64,161,128]{2,1,0:T(8,128)(2,1)} %pad_maximum_fusion), calls=%async_computation | async-start | bytes 5505024 | tf_op jit(solution)/shard_map/all_to_all | solution.py:84
  47.4 152.0 %all-gather.2.cloned.1.call-start = ((), (), s32[]{:S(2)}) async-start(), calls=%async_computation.3 | async-start | bytes 6553600 | tf_op jit(solution)/shard_map/all_gather | solution.py:34
  177.9 9.5 %collective-permute-start = (bf16[64,161,128]{2,0,1:T(8,128)(2,1)}, bf16[64,161,128]{2,0,1:T(8,128)(2,1)}, u32[]{:S(2)}, u32[]{:S(2)}) collective-permute-start(bf16[64,161,128]{2,0,1:T(8,128)(2,1)} %copy.68), channel_id=1, source_target_pairs={{0,4},{4,0},{1,5},{5,1},{2,6},{6,2},{3,7},{7,3},{8,12},{12,8},{9,1... | collective-permute-start | bytes 7913480 | tf_op jit(solution)/shard_map/ppermute | solution.py:111
  199.4 4.9 %copy-start.4 = (bf16[640,4096]{1,0:T(8,128)(2,1)S(1)}, bf16[640,4096]{1,0:T(8,128)(2,1)}, u32[]{:S(2)}) copy-start(bf16[640,4096]{1,0:T(8,128)(2,1)} %constant_dynamic-update-slice_fusion) | copy-start | bytes 15728644
  199.4 5.6 %copy-start.5 = (bf16[2,2048,640]{1,2,0:T(8,128)(2,1)S(1)}, bf16[2,2048,640]{1,2,0:T(8,128)(2,1)}, u32[]{:S(2)}) copy-start(bf16[2,2048,640]{1,2,0:T(8,128)(2,1)} %all-gather.2.cloned.1.call-done) | copy-start | bytes 15728644
  205.0 4.2 %copy-start.6 = (f32[640,640]{0,1:T(8,128)}, f32[640,640]{0,1:T(8,128)S(1)}, u32[]{:S(2)}) copy-start(f32[640,640]{0,1:T(8,128)S(1)} %fusion) | copy-start | bytes 4915204
  214.4 1.5 copy-start.3
  217.2 5.1 %collective-permute-start.1 = (bf16[64,81,128]{2,0,1:T(8,128)(2,1)S(1)}, bf16[64,81,128]{2,0,1:T(8,128)(2,1)S(1)}, u32[]{:S(2)}, u32[]{:S(2)}) collective-permute-start(bf16[64,81,128]{2,0,1:T(8,128)(2,1)S(1)} %pad_maximum_fusion.3), channel_id=1, source_target_pairs={{0,4},{4,0},{1,5},{5,1},{2,6},{6,2},{3,7},{7,3},{8,12},{12,8},{9,1... | collective-permute-start | bytes 3981320 | tf_op jit(solution)/shard_map/ppermute | solution.py:119
  234.8 78.5 %all-to-all-start.1 = ((bf16[64,81,128]{2,1,0:T(8,128)(2,1)}), bf16[64,81,128]{2,1,0:T(8,128)(2,1)S(1)}, u32[]{:S(2)}, u32[]{:S(2)}) async-start(bf16[64,81,128]{2,1,0:T(8,128)(2,1)} %pad_maximum_fusion.2), calls=%async_computation.1 | async-start | bytes 2883584 | tf_op jit(solution)/shard_map/all_to_all | solution.py:84
  240.6 82.0 %reduce-scatter.2.cloned.1.call-start = ((), (), s32[]{:S(2)}) async-start(), calls=%async_computation.4 | async-start | bytes 3276800 | tf_op jit(solution)/shard_map/reduce_scatter | solution.py:48
  320.8 1.9 copy-start.1
Sparse Core Ops, SparseCore 0:
  52.2 63.6 all-gather.1
  247.0 40.5 reduce-scatter.1

commit v5 on v4

--- a/solution.py
+++ b/solution.py
@@ -56,30 +56,6 @@
     return (token_part, gate_part, down_sum)
 
 
-def pack(rows, gate, experts):
-    count, row_width = rows.shape
-    per = count // experts
-    high, low = split_bf16(gate)
-    gate_row = jnp.concatenate(
-        [
-            high.reshape(experts, per),
-            low.reshape(experts, per),
-            jnp.zeros((experts, LANES - 2 * per), jnp.bfloat16),
-        ],
-        axis=1,
-    )
-    return jnp.concatenate(
-        [rows.reshape(experts, per * row_width // LANES, LANES), gate_row[:, None, :]], axis=1
-    )
-
-
-def unpack(packed, per):
-    experts = packed.shape[0]
-    body = packed[:, :-1].reshape(experts * per, -1)
-    gate_row = packed[:, -1].astype(jnp.float32)
-    return body, (gate_row[:, :per] + gate_row[:, per : 2 * per]).reshape(-1)
-
-
 def exchange(packed):
     return lax.all_to_all(packed, "epc", split_axis=0, concat_axis=0, tiled=True)
 
@@ -105,24 +81,32 @@
     send_x = jnp.where(is_valid[:, None], tokens[token_index], jnp.zeros((), tokens.dtype))
     send_dy = jnp.where(is_valid[:, None], cotangent[token_index], jnp.zeros((), cotangent.dtype))
     send_gate = jnp.where(is_valid, gate_values.reshape(-1)[assign], 0.0)
-    arrived = exchange(pack(jnp.concatenate([send_x, send_dy], axis=1), send_gate, experts))
+    pair_rows = jnp.concatenate([send_x, send_dy], axis=1)
+    arrived = exchange(pair_rows.reshape(experts, -1, LANES))
+    here = lax.axis_index("epc")
+    arrived_gate = lax.dynamic_slice_in_dim(
+        lax.all_gather(send_gate, "epc", axis=0, tiled=False), here * capacity, capacity, axis=1
+    ).reshape(-1)
+    arrived, arrived_gate = lax.optimization_barrier((arrived, arrived_gate))
     swap = [(0, 1), (1, 0)]
-    own_rows, own_gate = unpack(arrived, capacity)
-    partner_rows, partner_gate = unpack(lax.ppermute(arrived, "core", swap), capacity)
-    rows = jnp.concatenate([own_rows, partner_rows], axis=0)
-    rows_gate = jnp.concatenate([own_gate, partner_gate], axis=0)
+    rows = jnp.concatenate(
+        [arrived, lax.ppermute(arrived, "core", swap)], axis=0
+    ).reshape(2 * experts * capacity, 2 * width)
+    rows_gate = jnp.concatenate([arrived_gate, lax.ppermute(arrived_gate, "core", swap)], axis=0)
     token_part, gate_part, down_sum = expert_terms(
         rows[:, :width], rows[:, width:], rows_gate, up_weight, down_weight
     )
     own = experts * capacity
-    partner_token, partner_part = unpack(
-        lax.ppermute(pack(token_part[own:], gate_part[own:], experts), "core", swap), capacity
-    )
+    partner_token = lax.ppermute(token_part[own:], "core", swap)
+    partner_part = lax.ppermute(gate_part[own:], "core", swap)
     token_sum = (
         token_part[:own].astype(jnp.float32) + partner_token.astype(jnp.float32)
     ).astype(jnp.bfloat16)
     gate_sum = gate_part[:own] + partner_part
-    returned, returned_gate = unpack(exchange(pack(token_sum, gate_sum, experts)), capacity)
+    returned = exchange(token_sum.reshape(experts, -1, LANES)).reshape(experts * capacity, width)
+    returned_gate = lax.dynamic_slice_in_dim(
+        lax.all_gather(gate_sum, "epc", axis=0, tiled=False), here * capacity, capacity, axis=1
+    ).reshape(-1)
     pair = position.reshape(tok_rows, 2)
     token_grad = (
         returned[pair[:, 0]].astype(jnp.float32) + returned[pair[:, 1]].astype(jnp.float32)

time: 330 us -> 640 us (1.94)
  waiting for transfers between devices: 192 us -> 518 us
  local copies, waits for them, and re-layouts: 58.4 us -> 39.2 us
  starting transfers between devices: 29.2 us -> 37.2 us
    unnamed x2 -> x6, waiting for transfers between devices: 0.03 us -> 515 us
    all_to_all x2, waiting for transfers between devices: 190 us -> 0.01 us  [exchange(): lax.all_to_all(packed, 'epc', split_axis=0, concat_axis=0, tiled=True)]
    slice x10 -> x3, local copies, waits for them, and re-layouts: 9.01 us -> 0.39 us  [the longest x4 8.29 us: unpack(): body = packed[:, :-1].reshape(experts * per, -1)]
    reshape x12 -> x6, local copies, waits for them, and re-layouts: 17.2 us -> 14.3 us  [the longest x1 8.8 us: local(): rows = jnp.concatenate([arrived, lax.ppermute(arrived, 'core', swap)], ax...]
  transfers between devices with their start and end apart: 6 -> 10, of which waited for: 3 -> 4; matrix products, arithmetic and copies ran while one was open for 13% -> 6% of each run, Pallas kernels for 0% -> 0%
where the time goes in v5:
time: 640 us; the launch traced here: 638 us
  waiting for transfers between devices  518 us (81%)
  local copies, waits for them, and re-layouts  39.2 us (6%)
  starting transfers between devices  37.2 us (6%)
  between operations  16.5 us (3%)
  matrix products  16.4 us (3%)
  other arithmetic  11 us (2%)
    unnamed x6, waiting for transfers between devices  515 us
    all_to_all x2, starting transfers between devices, exchange(): lax.all_to_all(packed, 'epc', split_axis=0, concat_axis=0, tiled=True)  28 us
  transfers between devices with their start and end apart: 10, of which 4 were waited for; matrix products, arithmetic and copies ran while one was open for 6% of the time, Pallas kernels for 0%

profile of v5, /device:TPU:24, one launch (start us, length us, event | category | flops | bytes accessed | tf_op | source)
XLA Modules:
  0.0 638.4 jit_solution(11673911675517746560)
XLA Ops:
  10.4 1.4 scatter_custom_fusion
  11.9 2.4 gather_fusion
  14.4 3.0 gather_fusion.1
  17.4 1.6 broadcast_select_fusion.1
  19.1 3.1 reshape.88
  22.3 18.7 %all-to-all-start = ((bf16[64,160,128]{2,1,0:T(8,128)(2,1)}), bf16[64,160,128]{2,1,0:T(8,128)(2,1)S(1)}, u32[]{:S(2)}, u32[]{:S(2)}) async-start(bf16[64,160,128]{2,1,0:T(8,128)(2,1)} %reshape.88), calls=%async_computation | async-start | bytes 5242880 | tf_op jit(solution)/shard_map/all_to_all | solution.py:60
  41.3 2.5 gather_fusion.2
  43.8 1.3 dynamic-slice
  46.6 2.2 copy.22
  48.8 2.5 pad_maximum_fusion.2
  51.4 270.4 %all-reduce.7.cloned.1.call-done = f32[64,320]{1,0:T(8,128)} async-done(((f32[64,320]{1,0:T(8,128)}), f32[64,320]{1,0:T(8,128)}) %all-reduce.7.cloned.1.call-update) | async-done | bytes 81936
  321.8 0.9 constant_dynamic-slice_fusion.1
  322.9 1.9 collective-permute-start.1
  324.8 2.6 collective-permute-start
  327.4 2.3 collective-permute-done
  329.7 2.8 pad_maximum_fusion
  332.6 8.8 %reshape.91 = bf16[640,4096]{1,0:T(8,128)(2,1)} reshape(bf16[128,160,128]{2,1,0:T(8,128)(2,1)} %pad_maximum_fusion) | data formatting | bytes 10485760 | tf_op jit(solution)/shard_map/reshape | solution.py:94
  341.4 4.9 fusion
  347.0 2.4 multiply_reduce_fusion
  349.4 2.9 convolution_convert_fusion.1
  352.3 1.5 copy-done.3
  354.0 2.1 collective-permute-start.2
  356.1 2.3 collective-permute-start.3
  360.0 1.8 add_convert_fusion
  361.8 1.5 reshape.92
  363.3 9.3 %all-to-all-start.1 = ((bf16[64,80,128]{2,1,0:T(8,128)(2,1)}), bf16[64,80,128]{2,1,0:T(8,128)(2,1)S(1)}, u32[]{:S(2)}, u32[]{:S(2)}) async-start(bf16[64,80,128]{2,1,0:T(8,128)(2,1)} %reshape.92), calls=%async_computation.1 | async-start | bytes 2621440 | tf_op jit(solution)/shard_map/all_to_all | solution.py:60
  372.9 6.2 convolution_convert_fusion
  379.3 244.5 %all-reduce.9.cloned.1.call-done = f32[64,320]{1,0:T(8,128)} async-done(((f32[64,320]{1,0:T(8,128)}), f32[64,320]{1,0:T(8,128)}) %all-reduce.9.cloned.1.call-update) | async-done | bytes 81936
  624.8 1.9 gather_fusion.5
  628.2 0.9 gather_fusion.3
  629.1 0.9 gather_fusion.4
  630.1 0.9 add_convert_fusion.1
  (68 shorter events, 9.5 us)
Async XLA Ops:
  8.0 3.9 copy-start
  11.9 2.5 copy-start.1
  22.3 18.8 %copy-start.4 = (f32[128,2]{0,1:T(2,128)S(1)}, f32[128,2]{0,1:T(2,128)}, u32[]{:S(2)}) copy-start(f32[128,2]{0,1:T(2,128)} %param.9) | copy-start | bytes 3076
  22.3 300.6 %all-to-all-start = ((bf16[64,160,128]{2,1,0:T(8,128)(2,1)}), bf16[64,160,128]{2,1,0:T(8,128)(2,1)S(1)}, u32[]{:S(2)}, u32[]{:S(2)}) async-start(bf16[64,160,128]{2,1,0:T(8,128)(2,1)} %reshape.88), calls=%async_computation | async-start | bytes 5242880 | tf_op jit(solution)/shard_map/all_to_all | solution.py:60
  41.0 280.8 %all-reduce.7.cloned.1.call-start = ((), (), s32[]{:S(2)}) async-start(), calls=%async_computation.5 | async-start | bytes 196608
  46.6 294.8 %all-gather.4.cloned.1.call-start = ((), (), s32[]{:S(2)}) async-start(), calls=%async_computation.3 | async-start | bytes 6553600 | tf_op jit(solution)/shard_map/all_gather | solution.py:34
  51.3 572.5 %all-reduce.9.cloned.1.call-start = ((), (), s32[]{:S(2)}) async-start(), calls=%async_computation.6 | async-start | bytes 196608
  322.9 6.9 %collective-permute-start.1 = (bf16[64,160,128]{2,1,0:T(8,128)(2,1)S(1)}, bf16[64,160,128]{2,1,0:T(8,128)(2,1)S(1)}, u32[]{:S(2)}, u32[]{:S(2)}) collective-permute-start(bf16[64,160,128]{2,1,0:T(8,128)(2,1)S(1)} %all-to-all-done), channel_id=1, source_target_pairs={{0,4},{4,0},{1,5},{5,1},{2,6},{6,2},{3,7},{7,3},{8,12},{12,8},{9,1... | collective-permute-start | bytes 7864328 | tf_op jit(solution)/shard_map/ppermute | solution.py:93
  324.8 4.9 collective-permute-start
  341.4 4.9 copy-start.2
  341.4 5.6 copy-start.5
  347.0 2.4 copy-start.6
  352.3 1.5 copy-start.3
  354.0 6.1 collective-permute-start.2
  356.1 3.1 collective-permute-start.3
  363.3 264.3 %all-to-all-start.1 = ((bf16[64,80,128]{2,1,0:T(8,128)(2,1)}), bf16[64,80,128]{2,1,0:T(8,128)(2,1)S(1)}, u32[]{:S(2)}, u32[]{:S(2)}) async-start(bf16[64,80,128]{2,1,0:T(8,128)(2,1)} %reshape.92), calls=%async_computation.1 | async-start | bytes 2621440 | tf_op jit(solution)/shard_map/all_to_all | solution.py:60
  372.6 258.4 %reduce-scatter.2.cloned.1.call-start = ((), (), s32[]{:S(2)}) async-start(), calls=%async_computation.4 | async-start | bytes 3276800 | tf_op jit(solution)/shard_map/reduce_scatter | solution.py:48
Sparse Core Ops, SparseCore 0:
  46.7 275.0 all-reduce.6
  360.1 263.6 all-reduce.8
Sparse Core Ops, SparseCore 1:
  51.4 63.5 all-gather.3
  379.2 40.5 reduce-scatter.1

commit v6 on v3

--- a/solution.py
+++ b/solution.py
@@ -30,31 +30,30 @@
     return high, low
 
 
-def expert_terms(rows_x, rows_dy, rows_gate, up_weight, down_weight):
+def expert_terms(rows_x, rows_scaled, up_weight, down_weight):
     contract_last = (((1,), (1,)), ((), ()))
     both_full = lax.all_gather(
         jnp.stack([up_weight, down_weight.T]), "rep", axis=1, tiled=True
     )
     up_full = both_full[0]
     pre_act = jnp.dot(rows_x, up_full, preferred_element_type=jnp.float32)
-    grad_hidden = jnp.dot(rows_dy, both_full[1], preferred_element_type=jnp.float32)
+    gated_grad_hidden = jnp.dot(rows_scaled, both_full[1], preferred_element_type=jnp.float32)
     hidden = gelu_tanh(pre_act)
     hidden_bf = hidden.astype(jnp.bfloat16)
-    gate_part = jnp.sum(hidden * grad_hidden, axis=1)
-    scaled_dy = (rows_gate[:, None] * rows_dy.astype(jnp.float32)).astype(jnp.bfloat16)
+    gated_part = jnp.sum(hidden * gated_grad_hidden, axis=1)
     down_term = lax.dot_general(
-        hidden_bf, scaled_dy, (((0,), (0,)), ((), ())), preferred_element_type=jnp.float32
+        hidden_bf, rows_scaled, (((0,), (0,)), ((), ())), preferred_element_type=jnp.float32
     ).astype(jnp.bfloat16)
     down_sum = (
         lax.psum_scatter(down_term, "rep", scatter_dimension=1, tiled=True)
         .astype(jnp.float32)
         .astype(jnp.bfloat16)
     )
-    grad_pre = (rows_gate[:, None] * grad_hidden * gelu_slope(pre_act)).astype(jnp.bfloat16)
+    grad_pre = (gated_grad_hidden * gelu_slope(pre_act)).astype(jnp.bfloat16)
     token_part = lax.dot_general(
         grad_pre, up_full, contract_last, preferred_element_type=jnp.float32
     ).astype(jnp.bfloat16)
-    return (token_part, gate_part, down_sum)
+    return (token_part, gated_part, down_sum)
 
 
 def local(tokens, cotangent, expert_ids, gate_values, up_weight, down_weight):
@@ -76,14 +75,11 @@
     assign = jnp.where(is_valid, where_from, 0)
     token_index = assign // 2
     send_x = jnp.where(is_valid[:, None], tokens[token_index], jnp.zeros((), tokens.dtype))
-    send_dy = jnp.where(is_valid[:, None], cotangent[token_index], jnp.zeros((), cotangent.dtype))
     send_gate = jnp.where(is_valid, gate_values.reshape(-1)[assign], 0.0)
-    gate_high, gate_low = split_bf16(send_gate)
-    lane = jnp.arange(EXTRA, dtype=jnp.int32)[None, :]
-    extra = jnp.where(
-        lane == 0, gate_high[:, None], jnp.where(lane == 1, gate_low[:, None], jnp.zeros((), jnp.bfloat16))
+    send_scaled = (send_gate[:, None] * cotangent[token_index].astype(jnp.float32)).astype(
+        jnp.bfloat16
     )
-    send = jnp.concatenate([send_x, send_dy, extra], axis=1)
+    send = jnp.concatenate([send_x, send_scaled], axis=1)
     row_width = send.shape[1]
     arrived = lax.all_to_all(
         send.reshape(experts, capacity * row_width // LANES, LANES),
@@ -95,9 +91,8 @@
     swap = [(0, 1), (1, 0)]
     partner_rows = lax.ppermute(arrived, "core", swap)
     rows = jnp.concatenate([arrived, partner_rows], axis=0)
-    rows_gate = rows[:, 2 * width].astype(jnp.float32) + rows[:, 2 * width + 1].astype(jnp.float32)
     token_part, gate_part, down_sum = expert_terms(
-        rows[:, :width], rows[:, width : 2 * width], rows_gate, up_weight, down_weight
+        rows[:, :width], rows[:, width:], up_weight, down_weight
     )
     own = experts * capacity
     part_high, part_low = split_bf16(gate_part[own:])
@@ -133,7 +128,8 @@
     ).reshape(experts * capacity, back_width)
     picked = returned[position].astype(jnp.float32)
     token_grad = jnp.sum(picked[:, :width].reshape(tok_rows, 2, width), axis=1).astype(jnp.bfloat16)
-    gate_grad = (picked[:, width] + picked[:, width + 1]).reshape(tok_rows, 2)
+    gated_grad = picked[:, width] + picked[:, width + 1]
+    gate_grad = (gated_grad / gate_values.reshape(-1)).reshape(tok_rows, 2)
     return (token_grad, gate_grad, down_sum)
 
 

time: 309 us -> 303 us (0.981)
  waiting for transfers between devices: 196 us -> 189 us
    all_to_all x1, waiting for transfers between devices: 124 us -> 118 us  [local(): lax.all_to_all(send.reshape(experts, capacity * row_width // LANES, LANES...]
    unnamed x17 -> x15, local copies, waits for them, and re-layouts: 9.46 us -> 8.01 us
where the time goes in v6:
time: 303 us; the launch traced here: 302 us
  waiting for transfers between devices  189 us (62%)
  local copies, waits for them, and re-layouts  37.7 us (12%)
  starting transfers between devices  29.2 us (10%)
  matrix products  18.2 us (6%)
  between operations  14.4 us (5%)
  other arithmetic  13.6 us (4%)
    all_to_all x1, waiting for transfers between devices, local(): lax.all_to_all(send.reshape(experts, capacity * row_width // LANES, LANES...  118 us
    all_to_all x1, waiting for transfers between devices, local(): lax.all_to_all(back.reshape(experts, capacity * back_width // LANES, LANE...  66.5 us
    all_to_all x1, starting transfers between devices, local(): lax.all_to_all(send.reshape(experts, capacity * row_width // LANES, LANES...  18.6 us
    unnamed x15, local copies, waits for them, and re-layouts  8.01 us
    all_to_all x1, starting transfers between devices, local(): lax.all_to_all(back.reshape(experts, capacity * back_width // LANES, LANE...  6.19 us
  transfers between devices with their start and end apart: 6, of which 4 were waited for; matrix products, arithmetic and copies ran while one was open for 11% of the time, Pallas kernels for 0%

profile of v6, /device:TPU:24, one launch (start us, length us, event | category | flops | bytes accessed | tf_op | source)
XLA Modules:
  0.0 301.9 jit_solution(656041365353553732)
XLA Ops:
  7.2 0.8 copy.12
  10.2 1.4 scatter_custom_fusion
  12.6 2.5 gather_fusion.1
  15.1 2.4 gather_fusion.2
  17.6 3.0 %gather_fusion = bf16[320,2048]{1,0:T(8,128)(2,1)} fusion(bf16[128,2048]{1,0:T(8,128)(2,1)S(1)} %copy-done.1, s32[1024]{0:T(1024)S(1)} %get-tuple-element.15), kind=kCustom, calls=%fused_computation | custom fusion | bytes 2622720 | tf_op jit(solution)/shard_map/gather | solution.py:77
  20.6 1.5 broadcast_select_fusion
  22.6 3.1 %reshape.101 = bf16[64,160,128]{2,1,0:T(8,128)(2,1)} reshape(bf16[320,4096]{1,0:T(8,128)(2,1)S(1)} %pad_maximum_fusion) | data formatting | bytes 5242880 | tf_op jit(solution)/shard_map/reshape | solution.py:85
  25.7 18.6 %all-to-all-start = ((bf16[64,160,128]{2,1,0:T(8,128)(2,1)}), bf16[64,160,128]{2,1,0:T(8,128)(2,1)S(1)}, u32[]{:S(2)}, u32[]{:S(2)}) async-start(bf16[64,160,128]{2,1,0:T(8,128)(2,1)} %reshape.101), calls=%async_computation | async-start | bytes 5242880 | tf_op jit(solution)/shard_map/all_to_all | solution.py:84
  44.3 2.2 copy.16
  46.5 2.5 pad_maximum_fusion.3
  49.0 118.0 %all-to-all-done = bf16[64,160,128]{2,1,0:T(8,128)(2,1)S(1)} async-done(((bf16[64,160,128]{2,1,0:T(8,128)(2,1)}), bf16[64,160,128]{2,1,0:T(8,128)(2,1)S(1)}, u32[]{:S(2)}, u32[]{:S(2)}) %all-to-all-start) | async-done | bytes 2621472 | tf_op jit(solution)/shard_map/all_to_all | solution.py:84
  167.0 3.1 %reshape.102 = bf16[320,4096]{1,0:T(8,128)(2,1)} reshape(bf16[64,160,128]{2,1,0:T(8,128)(2,1)S(1)} %all-to-all-done) | data formatting | bytes 5242880 | tf_op jit(solution)/shard_map/reshape | solution.py:90
  170.1 2.1 collective-permute-start
  172.2 3.5 %constant_dynamic-update-slice_fusion.1 = bf16[640,4096]{1,0:T(8,128)(2,1)} fusion(bf16[320,4096]{1,0:T(8,128)(2,1)} %reshape.102), kind=kLoop, calls=%fused_computation.57 | loop fusion | bytes 5242880
  175.7 1.4 collective-permute-done
  177.1 1.9 constant_dynamic-update-slice_fusion
  179.0 4.9 %fusion = f32[640,640]{0,1:T(8,128)S(1)} fusion(bf16[640,4096]{1,0:T(8,128)(2,1)} %constant_dynamic-update-slice_fusion, bf16[2,2048,640]{1,2,0:T(8,128)(2,1)} %all-gather.2.cloned.1.call-done), kind=kOutput, calls=%fused_computation.8 | convolution fusion | flops 1677721600 | bytes 6881280 | tf_op jit(solution)/shard_map/dot_general | solution.py:39
  183.9 4.8 %multiply_reduce_fusion = (f32[640]{0:T(1024)S(1)}, f32[640,640]{0,1:T(8,128)S(1)}) fusion(f32[640,640]{0,1:T(8,128)S(1)} %fusion, bf16[2,2048,640]{1,2,0:T(8,128)(2,1)S(1)} %copy-done.2, bf16[640,4096]{1,0:T(8,128)(2,1)} %constant_dynamic-update-slice_fusion), kind=kOutput, calls=%fused_computation.26 | convolution fusion | flops 1681816960 | bytes 8522240 | tf_op jit(solution)/shard_map/dot_general | solution.py:40
  188.7 2.9 convolution_convert_fusion.1
  192.1 2.0 collective-permute-start.1
  194.2 3.0 collective-permute-done.1
  198.1 2.5 reshape.103
  200.6 6.2 %all-to-all-start.1 = ((bf16[64,85,128]{2,1,0:T(8,128)(2,1)}), bf16[64,85,128]{2,1,0:T(8,128)(2,1)}, u32[]{:S(2)}, u32[]{:S(2)}) async-start(bf16[64,85,128]{2,1,0:T(8,128)(2,1)} %reshape.103), calls=%async_computation.1 | async-start | bytes 2883584 | tf_op jit(solution)/shard_map/all_to_all | solution.py:122
  207.0 5.5 %convolution_convert_fusion = bf16[640,2048]{1,0:T(8,128)(2,1)} fusion(bf16[640,4096]{1,0:T(8,128)(2,1)} %constant_dynamic-update-slice_fusion, f32[640,640]{0,1:T(8,128)S(1)} %copy-done.4), kind=kOutput, calls=%fused_computation.5 | convolution fusion | flops 1682718720 | bytes 6881280 | tf_op jit(solution)/shard_map/dot_general | solution.py:44
  212.6 66.5 %all-to-all-done.1 = bf16[64,85,128]{2,1,0:T(8,128)(2,1)} async-done(((bf16[64,85,128]{2,1,0:T(8,128)(2,1)}), bf16[64,85,128]{2,1,0:T(8,128)(2,1)}, u32[]{:S(2)}, u32[]{:S(2)}) %all-to-all-start.1) | async-done | bytes 1392672 | tf_op jit(solution)/shard_map/all_to_all | solution.py:122
  279.1 3.1 %reshape.104 = bf16[320,2176]{1,0:T(8,128)(2,1)S(1)} reshape(bf16[64,85,128]{2,1,0:T(8,128)(2,1)} %all-to-all-done.1) | data formatting | bytes 2785280 | tf_op jit(solution)/shard_map/reshape | solution.py:128
  282.1 1.5 gather_fusion.3
  283.7 1.6 slice.82
  285.3 1.5 convert_element_type.82
  286.8 2.5 reshape.105
  289.3 1.2 fusion.19
  291.3 3.8 %reduce_sum.29 = bf16[128,2048]{1,0:T(8,128)(2,1)} reduce(f32[128,2,2048]{2,1,0:T(2,128)S(1)} %reshape.105, f32[]{:T(128)} %constant.22.clone.1), dimensions={1}, to_apply=%region_5.6 | reduce | flops 262144 | bytes 2621444 | tf_op jit(solution)/shard_map/reduce_sum | solution.py:130
  (52 shorter events, 6.1 us)
Async XLA Ops:
  7.2 7.9 %copy-start = (bf16[128,2048]{1,0:T(8,128)(2,1)S(1)}, bf16[128,2048]{1,0:T(8,128)(2,1)}, u32[]{:S(2)}) copy-start(bf16[128,2048]{1,0:T(8,128)(2,1)} %param.7) | copy-start | bytes 1572868
  15.1 2.5 copy-start.1
  25.7 141.3 %all-to-all-start = ((bf16[64,160,128]{2,1,0:T(8,128)(2,1)}), bf16[64,160,128]{2,1,0:T(8,128)(2,1)S(1)}, u32[]{:S(2)}, u32[]{:S(2)}) async-start(bf16[64,160,128]{2,1,0:T(8,128)(2,1)} %reshape.101), calls=%async_computation | async-start | bytes 5242880 | tf_op jit(solution)/shard_map/all_to_all | solution.py:84
  44.3 134.7 %all-gather.2.cloned.1.call-start = ((), (), s32[]{:S(2)}) async-start(), calls=%async_computation.3 | async-start | bytes 6553600 | tf_op jit(solution)/shard_map/all_gather | solution.py:35
  170.1 7.0 %collective-permute-start = (bf16[320,4096]{1,0:T(8,128)(2,1)}, bf16[320,4096]{1,0:T(8,128)(2,1)S(1)}, u32[]{:S(2)}, u32[]{:S(2)}) collective-permute-start(bf16[320,4096]{1,0:T(8,128)(2,1)} %reshape.102), channel_id=1, source_target_pairs={{0,4},{4,0},{1,5},{5,1},{2,6},{6,2},{3,7},{7,3},{8,12},{12,8},{9,1... | collective-permute-start | bytes 7864328 | tf_op jit(solution)/shard_map/ppermute | solution.py:92
  179.0 4.9 %copy-start.2 = (bf16[2,2048,640]{1,2,0:T(8,128)(2,1)S(1)}, bf16[2,2048,640]{1,2,0:T(8,128)(2,1)}, u32[]{:S(2)}) copy-start(bf16[2,2048,640]{1,2,0:T(8,128)(2,1)} %all-gather.2.cloned.1.call-done) | copy-start | bytes 15728644
  183.9 4.8 %copy-start.3 = (f32[640,640]{0,1:T(8,128)}, f32[640,640]{0,1:T(8,128)S(1)}, u32[]{:S(2)}) copy-start(f32[640,640]{0,1:T(8,128)S(1)} %fusion) | copy-start | bytes 4915204
  192.1 5.0 %collective-permute-start.1 = (bf16[320,2176]{1,0:T(8,128)(2,1)S(1)}, bf16[320,2176]{1,0:T(8,128)(2,1)S(1)}, u32[]{:S(2)}, u32[]{:S(2)}) collective-permute-start(bf16[320,2176]{1,0:T(8,128)(2,1)S(1)} %pad_maximum_fusion.1), channel_id=1, source_target_pairs={{0,4},{4,0},{1,5},{5,1},{2,6},{6,2},{3,7},{7,3},{8,12},{12,8},{9,1... | collective-permute-start | bytes 4177928 | tf_op jit(solution)/shard_map/ppermute | solution.py:105
  200.6 6.5 %copy-start.4 = (f32[640,640]{0,1:T(8,128)S(1)}, f32[640,640]{0,1:T(8,128)}, u32[]{:S(2)}) copy-start(f32[640,640]{0,1:T(8,128)} %copy-done.3) | copy-start | bytes 4915204
  200.6 78.5 %all-to-all-start.1 = ((bf16[64,85,128]{2,1,0:T(8,128)(2,1)}), bf16[64,85,128]{2,1,0:T(8,128)(2,1)}, u32[]{:S(2)}, u32[]{:S(2)}) async-start(bf16[64,85,128]{2,1,0:T(8,128)(2,1)} %reshape.103), calls=%async_computation.1 | async-start | bytes 2883584 | tf_op jit(solution)/shard_map/all_to_all | solution.py:122
  206.8 88.3 %reduce-scatter.2.cloned.1.call-start = ((), (), s32[]{:S(2)}) async-start(), calls=%async_computation.4 | async-start | bytes 3276800 | tf_op jit(solution)/shard_map/reduce_scatter | solution.py:48
Sparse Core Ops, SparseCore 0:
  49.1 63.6 all-gather.1
  212.7 40.4 reduce-scatter.1

commit v7 on v6

--- a/solution.py
+++ b/solution.py
@@ -126,9 +126,15 @@
         concat_axis=0,
         tiled=True,
     ).reshape(experts * capacity, back_width)
-    picked = returned[position].astype(jnp.float32)
-    token_grad = jnp.sum(picked[:, :width].reshape(tok_rows, 2, width), axis=1).astype(jnp.bfloat16)
-    gated_grad = picked[:, width] + picked[:, width + 1]
+    slots = jnp.arange(experts * capacity, dtype=jnp.int32)[None, None, :]
+    select = jnp.any(position.reshape(tok_rows, 2)[:, :, None] == slots, axis=1)
+    token_grad = jnp.dot(
+        select.astype(jnp.bfloat16), returned[:, :width], preferred_element_type=jnp.float32
+    ).astype(jnp.bfloat16)
+    returned_gate = returned[:, width].astype(jnp.float32) + returned[:, width + 1].astype(
+        jnp.float32
+    )
+    gated_grad = returned_gate[position]
     gate_grad = (gated_grad / gate_values.reshape(-1)).reshape(tok_rows, 2)
     return (token_grad, gate_grad, down_sum)
 

time: 303 us -> 291 us (0.960)
  other arithmetic: 13.6 us -> 6.49 us
  local copies, waits for them, and re-layouts: 37.7 us -> 32.4 us
    reduce_sum x1 -> x0, other arithmetic: 3.77 us -> none  [local(): jnp.sum(picked[:, :width].reshape(tok_rows, 2, width), axis=1)]
    unnamed x15 -> x17, local copies, waits for them, and re-layouts: 8.01 us -> 8.35 us
  transfers between devices with their start and end apart: 6 -> 6, of which waited for: 4 -> 4; matrix products, arithmetic and copies ran while one was open for 11% -> 9% of each run, Pallas kernels for 0% -> 0%
where the time goes in v7:
time: 291 us; the launch traced here: 290 us
  waiting for transfers between devices  188 us (65%)
  local copies, waits for them, and re-layouts  32.4 us (11%)
  starting transfers between devices  28.8 us (10%)
  matrix products  19.8 us (7%)
  between operations  14.4 us (5%)
  other arithmetic  6.49 us (2%)
    all_to_all x1, waiting for transfers between devices, local(): lax.all_to_all(send.reshape(experts, capacity * row_width // LANES, LANES...  118 us
    all_to_all x1, waiting for transfers between devices, local(): lax.all_to_all(back.reshape(experts, capacity * back_width // LANES, LANE...  66 us
    all_to_all x1, starting transfers between devices, local(): lax.all_to_all(send.reshape(experts, capacity * row_width // LANES, LANES...  18.6 us
    unnamed x17, local copies, waits for them, and re-layouts  8.35 us
    dot_general x1, matrix products, expert_terms(): lax.dot_general(hidden_bf, rows_scaled, (((0,), (0,)), ((), ())), preferr...  6.03 us
    all_to_all x1, starting transfers between devices, local(): lax.all_to_all(back.reshape(experts, capacity * back_width // LANES, LANE...  5.82 us
  transfers between devices with their start and end apart: 6, of which 4 were waited for; matrix products, arithmetic and copies ran while one was open for 9% of the time, Pallas kernels for 0%

profile of v7, /device:TPU:24, one launch (start us, length us, event | category | flops | bytes accessed | tf_op | source)
XLA Modules:
  0.0 290.3 jit_solution(7960607969707046026)
XLA Ops:
  7.2 0.8 copy.19
  8.3 0.6 reduce-window.6
  9.6 1.4 scatter_custom_fusion
  11.1 2.4 gather_fusion
  13.5 1.2 broadcast_select_fusion
  15.0 2.5 gather_fusion.1
  17.5 2.4 gather_fusion.2
  20.2 1.0 copy-done.2
  21.4 3.1 %reshape.108 = bf16[64,160,128]{2,1,0:T(8,128)(2,1)} reshape(bf16[320,4096]{1,0:T(8,128)(2,1)S(1)} %pad_maximum_fusion) | data formatting | bytes 5242880 | tf_op jit(solution)/shard_map/reshape | solution.py:85
  24.6 18.6 %all-to-all-start = ((bf16[64,160,128]{2,1,0:T(8,128)(2,1)}), bf16[64,160,128]{2,1,0:T(8,128)(2,1)S(1)}, u32[]{:S(2)}, u32[]{:S(2)}) async-start(bf16[64,160,128]{2,1,0:T(8,128)(2,1)} %reshape.108), calls=%async_computation | async-start | bytes 5242880 | tf_op jit(solution)/shard_map/all_to_all | solution.py:84
  43.2 2.2 copy.25
  45.4 2.5 pad_maximum_fusion.3
  47.9 118.0 %all-to-all-done = bf16[64,160,128]{2,1,0:T(8,128)(2,1)S(1)} async-done(((bf16[64,160,128]{2,1,0:T(8,128)(2,1)}), bf16[64,160,128]{2,1,0:T(8,128)(2,1)S(1)}, u32[]{:S(2)}, u32[]{:S(2)}) %all-to-all-start) | async-done | bytes 2621472 | tf_op jit(solution)/shard_map/all_to_all | solution.py:84
  165.8 3.1 %reshape.109 = bf16[320,4096]{1,0:T(8,128)(2,1)} reshape(bf16[64,160,128]{2,1,0:T(8,128)(2,1)S(1)} %all-to-all-done) | data formatting | bytes 5242880 | tf_op jit(solution)/shard_map/reshape | solution.py:90
  169.0 2.1 collective-permute-start
  171.1 3.5 %constant_dynamic-update-slice_fusion.1 = bf16[640,4096]{1,0:T(8,128)(2,1)} fusion(bf16[320,4096]{1,0:T(8,128)(2,1)} %reshape.109), kind=kLoop, calls=%fused_computation.61 | loop fusion | bytes 5242880
  174.6 1.4 collective-permute-done
  176.0 1.9 constant_dynamic-update-slice_fusion
  177.8 4.9 %fusion = f32[640,640]{0,1:T(8,128)S(1)} fusion(bf16[640,4096]{1,0:T(8,128)(2,1)} %constant_dynamic-update-slice_fusion, bf16[2,2048,640]{1,2,0:T(8,128)(2,1)} %all-gather.2.cloned.1.call-done), kind=kOutput, calls=%fused_computation.8 | convolution fusion | flops 1677721600 | bytes 6881280 | tf_op jit(solution)/shard_map/dot_general | solution.py:39
  182.8 4.7 %multiply_reduce_fusion = (f32[640]{0:T(1024)S(1)}, f32[640,640]{0,1:T(8,128)S(1)}) fusion(f32[640,640]{0,1:T(8,128)S(1)} %fusion, bf16[2,2048,640]{1,2,0:T(8,128)(2,1)S(1)} %copy-done.4, bf16[640,4096]{1,0:T(8,128)(2,1)} %constant_dynamic-update-slice_fusion), kind=kOutput, calls=%fused_computation.27 | convolution fusion | flops 1681816960 | bytes 8522240 | tf_op jit(solution)/shard_map/dot_general | solution.py:40
  187.5 2.9 convolution_convert_fusion.1
  190.9 2.0 collective-permute-start.1
  192.9 3.0 %collective-permute-done.1 = bf16[320,2176]{1,0:T(8,128)(2,1)S(1)} collective-permute-done((bf16[320,2176]{1,0:T(8,128)(2,1)S(1)}, bf16[320,2176]{1,0:T(8,128)(2,1)S(1)}, u32[]{:S(2)}, u32[]{:S(2)}) %collective-permute-start.1) | collective-permute-done | bytes 1392672 | tf_op jit(solution)/shard_map/ppermute | solution.py:105
  196.3 0.4 add_convert_fusion
  196.9 2.5 reshape.110
  199.3 5.8 %all-to-all-start.1 = ((bf16[64,85,128]{2,1,0:T(8,128)(2,1)}), bf16[64,85,128]{2,1,0:T(8,128)(2,1)S(1)}, u32[]{:S(2)}, u32[]{:S(2)}) async-start(bf16[64,85,128]{2,1,0:T(8,128)(2,1)} %reshape.110), calls=%async_computation.1 | async-start | bytes 2883584 | tf_op jit(solution)/shard_map/all_to_all | solution.py:122
  205.4 6.0 %convolution_convert_fusion = bf16[640,2048]{1,0:T(8,128)(2,1)} fusion(bf16[640,4096]{1,0:T(8,128)(2,1)} %constant_dynamic-update-slice_fusion, f32[640,640]{0,1:T(8,128)} %copy-done.5), kind=kOutput, calls=%fused_computation.5 | convolution fusion | flops 1682718720 | bytes 6881280 | tf_op jit(solution)/shard_map/dot_general | solution.py:44
  211.6 66.0 %all-to-all-done.1 = bf16[64,85,128]{2,1,0:T(8,128)(2,1)S(1)} async-done(((bf16[64,85,128]{2,1,0:T(8,128)(2,1)}), bf16[64,85,128]{2,1,0:T(8,128)(2,1)S(1)}, u32[]{:S(2)}, u32[]{:S(2)}) %all-to-all-start.1) | async-done | bytes 1392672 | tf_op jit(solution)/shard_map/all_to_all | solution.py:122
  277.6 1.6 reshape.111
  279.4 2.0 gather_fusion.3
  281.5 0.6 copy.27
  282.2 1.3 convolution_convert_fusion.2
  (53 shorter events, 3.5 us)
Async XLA Ops:
  7.2 3.9 %copy-start = (bf16[128,2048]{1,0:T(8,128)(2,1)S(1)}, bf16[128,2048]{1,0:T(8,128)(2,1)}, u32[]{:S(2)}) copy-start(bf16[128,2048]{1,0:T(8,128)(2,1)} %param.6) | copy-start | bytes 1572868
  13.5 1.2 copy-start.3
  14.8 2.7 copy-start.1
  19.9 1.3 copy-start.2
  24.6 141.3 %all-to-all-start = ((bf16[64,160,128]{2,1,0:T(8,128)(2,1)}), bf16[64,160,128]{2,1,0:T(8,128)(2,1)S(1)}, u32[]{:S(2)}, u32[]{:S(2)}) async-start(bf16[64,160,128]{2,1,0:T(8,128)(2,1)} %reshape.108), calls=%async_computation | async-start | bytes 5242880 | tf_op jit(solution)/shard_map/all_to_all | solution.py:84
  43.1 134.7 %all-gather.2.cloned.1.call-start = ((), (), s32[]{:S(2)}) async-start(), calls=%async_computation.3 | async-start | bytes 6553600 | tf_op jit(solution)/shard_map/all_gather | solution.py:35
  169.0 7.0 %collective-permute-start = (bf16[320,4096]{1,0:T(8,128)(2,1)}, bf16[320,4096]{1,0:T(8,128)(2,1)S(1)}, u32[]{:S(2)}, u32[]{:S(2)}) collective-permute-start(bf16[320,4096]{1,0:T(8,128)(2,1)} %reshape.109), channel_id=1, source_target_pairs={{0,4},{4,0},{1,5},{5,1},{2,6},{6,2},{3,7},{7,3},{8,12},{12,8},{9,1... | collective-permute-start | bytes 7864328 | tf_op jit(solution)/shard_map/ppermute | solution.py:92
  177.8 4.9 %copy-start.4 = (bf16[2,2048,640]{1,2,0:T(8,128)(2,1)S(1)}, bf16[2,2048,640]{1,2,0:T(8,128)(2,1)}, u32[]{:S(2)}) copy-start(bf16[2,2048,640]{1,2,0:T(8,128)(2,1)} %all-gather.2.cloned.1.call-done) | copy-start | bytes 15728644
  182.8 4.7 %copy-start.5 = (f32[640,640]{0,1:T(8,128)}, f32[640,640]{0,1:T(8,128)S(1)}, u32[]{:S(2)}) copy-start(f32[640,640]{0,1:T(8,128)S(1)} %fusion) | copy-start | bytes 4915204
  190.9 5.0 %collective-permute-start.1 = (bf16[320,2176]{1,0:T(8,128)(2,1)S(1)}, bf16[320,2176]{1,0:T(8,128)(2,1)S(1)}, u32[]{:S(2)}, u32[]{:S(2)}) collective-permute-start(bf16[320,2176]{1,0:T(8,128)(2,1)S(1)} %pad_maximum_fusion.1), channel_id=1, source_target_pairs={{0,4},{4,0},{1,5},{5,1},{2,6},{6,2},{3,7},{7,3},{8,12},{12,8},{9,1... | collective-permute-start | bytes 4177928 | tf_op jit(solution)/shard_map/ppermute | solution.py:105
  199.3 78.3 %all-to-all-start.1 = ((bf16[64,85,128]{2,1,0:T(8,128)(2,1)}), bf16[64,85,128]{2,1,0:T(8,128)(2,1)S(1)}, u32[]{:S(2)}, u32[]{:S(2)}) async-start(bf16[64,85,128]{2,1,0:T(8,128)(2,1)} %reshape.110), calls=%async_computation.1 | async-start | bytes 2883584 | tf_op jit(solution)/shard_map/all_to_all | solution.py:122
  205.1 78.3 %reduce-scatter.2.cloned.1.call-start = ((), (), s32[]{:S(2)}) async-start(), calls=%async_computation.4 | async-start | bytes 3276800 | tf_op jit(solution)/shard_map/reduce_scatter | solution.py:48
Sparse Core Ops, SparseCore 0:
  48.0 63.6 all-gather.1
  211.6 40.5 reduce-scatter.1

commit v8 on v7

--- a/solution.py
+++ b/solution.py
@@ -30,30 +30,21 @@
     return high, low
 
 
-def expert_terms(rows_x, rows_scaled, up_weight, down_weight):
+def expert_terms(rows_x, rows_scaled, up_full, down_full_t):
     contract_last = (((1,), (1,)), ((), ()))
-    both_full = lax.all_gather(
-        jnp.stack([up_weight, down_weight.T]), "rep", axis=1, tiled=True
-    )
-    up_full = both_full[0]
     pre_act = jnp.dot(rows_x, up_full, preferred_element_type=jnp.float32)
-    gated_grad_hidden = jnp.dot(rows_scaled, both_full[1], preferred_element_type=jnp.float32)
+    gated_grad_hidden = jnp.dot(rows_scaled, down_full_t, preferred_element_type=jnp.float32)
     hidden = gelu_tanh(pre_act)
     hidden_bf = hidden.astype(jnp.bfloat16)
     gated_part = jnp.sum(hidden * gated_grad_hidden, axis=1)
     down_term = lax.dot_general(
         hidden_bf, rows_scaled, (((0,), (0,)), ((), ())), preferred_element_type=jnp.float32
-    ).astype(jnp.bfloat16)
-    down_sum = (
-        lax.psum_scatter(down_term, "rep", scatter_dimension=1, tiled=True)
-        .astype(jnp.float32)
-        .astype(jnp.bfloat16)
     )
     grad_pre = (gated_grad_hidden * gelu_slope(pre_act)).astype(jnp.bfloat16)
     token_part = lax.dot_general(
         grad_pre, up_full, contract_last, preferred_element_type=jnp.float32
     ).astype(jnp.bfloat16)
-    return (token_part, gated_part, down_sum)
+    return (token_part, gated_part, down_term)
 
 
 def local(tokens, cotangent, expert_ids, gate_values, up_weight, down_weight):
@@ -90,12 +81,21 @@
     ).reshape(experts * capacity, row_width)
     swap = [(0, 1), (1, 0)]
     partner_rows = lax.ppermute(arrived, "core", swap)
-    rows = jnp.concatenate([arrived, partner_rows], axis=0)
-    token_part, gate_part, down_sum = expert_terms(
-        rows[:, :width], rows[:, width:], up_weight, down_weight
+    both_full = lax.all_gather(
+        jnp.stack([up_weight, down_weight.T]), "rep", axis=1, tiled=True
     )
-    own = experts * capacity
-    part_high, part_low = split_bf16(gate_part[own:])
+    own_token, own_gate, own_down = expert_terms(
+        arrived[:, :width], arrived[:, width:], both_full[0], both_full[1]
+    )
+    other_token, other_gate, other_down = expert_terms(
+        partner_rows[:, :width], partner_rows[:, width:], both_full[0], both_full[1]
+    )
+    down_sum = (
+        lax.psum_scatter((own_down + other_down).astype(jnp.bfloat16), "rep", scatter_dimension=1, tiled=True)
+        .astype(jnp.float32)
+        .astype(jnp.bfloat16)
+    )
+    part_high, part_low = split_bf16(other_gate)
     back_lane = jnp.arange(EXTRA, dtype=jnp.int32)[None, :]
     back_extra = jnp.where(
         back_lane == 0,
@@ -103,12 +103,12 @@
         jnp.where(back_lane == 1, part_low[:, None], jnp.zeros((), jnp.bfloat16)),
     )
     partner_back = lax.ppermute(
-        jnp.concatenate([token_part[own:], back_extra], axis=1), "core", swap
+        jnp.concatenate([other_token, back_extra], axis=1), "core", swap
     )
     token_sum = (
-        token_part[:own].astype(jnp.float32) + partner_back[:, :width].astype(jnp.float32)
+        own_token.astype(jnp.float32) + partner_back[:, :width].astype(jnp.float32)
     ).astype(jnp.bfloat16)
-    gate_sum = gate_part[:own] + (
+    gate_sum = own_gate + (
         partner_back[:, width].astype(jnp.float32) + partner_back[:, width + 1].astype(jnp.float32)
     )
     sum_high, sum_low = split_bf16(gate_sum)

time: 291 us -> 294 us (1.010)
    ppermute x1, waiting for transfers between devices: 1.35 us -> 5.04 us  [local(): partner_rows = lax.ppermute(arrived, 'core', swap)]
    ppermute x1, waiting for transfers between devices: 3 us -> 0.01 us  [local(): lax.ppermute(jnp.concatenate([other_token, back_extra], axis=1), 'core',...]
    unnamed x17 -> x26, local copies, waits for them, and re-layouts: 8.35 us -> 5.77 us
    dot_general x1 -> x2, matrix products: 6.03 us -> 6.11 us  [expert_terms(): lax.dot_general(hidden_bf, rows_scaled, (((0,), (0,)), ((), ())), preferr...]
  transfers between devices with their start and end apart: 6 -> 6, of which waited for: 4 -> 3; matrix products, arithmetic and copies ran while one was open for 9% -> 8% of each run, Pallas kernels for 0% -> 0%
where the time goes in v8:
time: 294 us; the launch traced here: 293 us
  waiting for transfers between devices  189 us (64%)
  local copies, waits for them, and re-layouts  31.6 us (11%)
  starting transfers between devices  29 us (10%)
  matrix products  21.6 us (7%)
  between operations  14.5 us (5%)
  other arithmetic  7.2 us (2%)
    all_to_all x1, waiting for transfers between devices, local(): lax.all_to_all(send.reshape(experts, capacity * row_width // LANES, LANES...  118 us
    all_to_all x1, waiting for transfers between devices, local(): lax.all_to_all(back.reshape(experts, capacity * back_width // LANES, LANE...  66.2 us
    all_to_all x1, starting transfers between devices, local(): lax.all_to_all(send.reshape(experts, capacity * row_width // LANES, LANES...  18.6 us
    dot_general x2, matrix products, expert_terms(): lax.dot_general(hidden_bf, rows_scaled, (((0,), (0,)), ((), ())), preferr...  6.11 us
    all_to_all x1, starting transfers between devices, local(): lax.all_to_all(back.reshape(experts, capacity * back_width // LANES, LANE...  6.08 us
  transfers between devices with their start and end apart: 6, of which 3 were waited for; matrix products, arithmetic and copies ran while one was open for 8% of the time, Pallas kernels for 0%

profile of v8, /device:TPU:24, one launch (start us, length us, event | category | flops | bytes accessed | tf_op | source)
XLA Modules:
  0.0 293.1 jit_solution(15963410409102040357)
XLA Ops:
  7.2 0.8 copy.42
  9.6 1.4 scatter_custom_fusion
  11.1 0.8 copy.47
  12.0 2.5 gather_fusion.1
  14.5 2.4 gather_fusion.2
  17.0 3.0 %gather_fusion = bf16[320,2048]{1,0:T(8,128)(2,1)} fusion(bf16[128,2048]{1,0:T(8,128)(2,1)S(1)} %copy-done.1, s32[1024]{0:T(1024)S(1)} %pad_clamp_fusion.2), kind=kCustom, calls=%fused_computation | custom fusion | bytes 2622720 | tf_op jit(solution)/shard_map/gather | solution.py:68
  20.0 1.5 broadcast_select_fusion
  21.9 3.2 %reshape.111 = bf16[64,160,128]{2,1,0:T(8,128)(2,1)} reshape(bf16[320,4096]{1,0:T(8,128)(2,1)S(1)} %pad_maximum_fusion) | data formatting | bytes 5242880 | tf_op jit(solution)/shard_map/reshape | solution.py:76
  25.1 18.6 %all-to-all-start = ((bf16[64,160,128]{2,1,0:T(8,128)(2,1)}), bf16[64,160,128]{2,1,0:T(8,128)(2,1)S(1)}, u32[]{:S(2)}, u32[]{:S(2)}) async-start(bf16[64,160,128]{2,1,0:T(8,128)(2,1)} %reshape.111), calls=%async_computation | async-start | bytes 5242880 | tf_op jit(solution)/shard_map/all_to_all | solution.py:75
  43.7 2.2 copy.48
  45.9 2.5 pad_maximum_fusion.3
  48.4 118.0 %all-to-all-done = bf16[64,160,128]{2,1,0:T(8,128)(2,1)S(1)} async-done(((bf16[64,160,128]{2,1,0:T(8,128)(2,1)}), bf16[64,160,128]{2,1,0:T(8,128)(2,1)S(1)}, u32[]{:S(2)}, u32[]{:S(2)}) %all-to-all-start) | async-done | bytes 2621472 | tf_op jit(solution)/shard_map/all_to_all | solution.py:75
  166.4 3.1 %reshape.112 = bf16[320,4096]{1,0:T(8,128)(2,1)} reshape(bf16[64,160,128]{2,1,0:T(8,128)(2,1)S(1)} %all-to-all-done) | data formatting | bytes 5242880 | tf_op jit(solution)/shard_map/reshape | solution.py:81
  169.5 1.9 collective-permute-start
  171.5 5.0 %collective-permute-done = bf16[320,4096]{1,0:T(8,128)(2,1)S(1)} collective-permute-done((bf16[320,4096]{1,0:T(8,128)(2,1)}, bf16[320,4096]{1,0:T(8,128)(2,1)S(1)}, u32[]{:S(2)}, u32[]{:S(2)}) %collective-permute-start) | collective-permute-done | bytes 2621472 | tf_op jit(solution)/shard_map/ppermute | solution.py:83
  176.5 3.9 %fusion.3 = f32[320,640]{1,0:T(8,128)S(1)} fusion(bf16[2,2048,640]{1,2,0:T(8,128)(2,1)} %all-gather.2.cloned.1.call-done, bf16[320,4096]{1,0:T(8,128)(2,1)S(1)} %collective-permute-done), kind=kOutput, calls=%fused_computation.17 | convolution fusion | flops 838860800 | bytes 4751360 | tf_op jit(solution)/shard_map/dot_general | solution.py:35
  180.5 1.4 multiply_reduce_fusion.1
  182.0 1.5 convolution_convert_fusion
  183.6 2.4 collective-permute-start.1
  186.0 1.2 fusion.4
  187.3 2.2 multiply_reduce_fusion
  189.4 1.1 copy-done.8
  191.0 4.1 %add_convert_fusion.1 = bf16[320,2048]{1,0:T(8,128)(2,1)S(1)} fusion(bf16[320,2176]{1,0:T(8,128)(2,1)} %copy-done.8, bf16[2,2048,640]{1,2,0:T(8,128)(2,1)} %all-gather.2.cloned.1.call-done, f32[320,640]{1,0:T(8,128)} %get-tuple-element.28, f32[320,640]{1,0:T(8,128)} %copy-done.3), kind=kOutput, calls=%fused_computation.12 | convolution fusion | flops 846028800 | bytes 6881280 | tf_op jit(solution)/shard_map/dot_general | solution.py:44
  195.1 1.2 pad_maximum_fusion.2
  196.3 4.0 %reshape.113 = bf16[64,85,128]{2,1,0:T(8,128)(2,1)} reshape(bf16[320,2176]{1,0:T(8,128)(2,1)} %pad_maximum_fusion.2) | data formatting | bytes 2785280 | tf_op jit(solution)/shard_map/reshape | solution.py:123
  200.4 6.1 %all-to-all-start.1 = ((bf16[64,85,128]{2,1,0:T(8,128)(2,1)}), bf16[64,85,128]{2,1,0:T(8,128)(2,1)}, u32[]{:S(2)}, u32[]{:S(2)}) async-start(bf16[64,85,128]{2,1,0:T(8,128)(2,1)} %reshape.113), calls=%async_computation.1 | async-start | bytes 2883584 | tf_op jit(solution)/shard_map/all_to_all | solution.py:122
  206.5 2.9 %fusion.10 = f32[640,2048]{1,0:T(8,128)S(1)} fusion(bf16[320,4096]{1,0:T(8,128)(2,1)S(1)} %copy-done.2, f32[320,640]{1,0:T(8,128)} %copy-done.3), kind=kOutput, calls=%fused_computation.32 | convolution fusion | flops 840704000 | bytes 7372800 | tf_op jit(solution)/shard_map/dot_general | solution.py:40
  209.5 3.2 %add_convert_fusion = bf16[640,2048]{1,0:T(8,128)(2,1)} fusion(f32[640,2048]{1,0:T(8,128)S(1)} %fusion.10, bf16[320,4096]{1,0:T(8,128)(2,1)S(1)} %copy-done.7, f32[320,640]{1,0:T(8,128)S(1)} %copy-done.5), kind=kOutput, calls=%fused_computation.5 | convolution fusion | flops 843325440 | bytes 9994240 | tf_op jit(solution)/shard_map/dot_general | solution.py:40
  212.8 66.2 %all-to-all-done.1 = bf16[64,85,128]{2,1,0:T(8,128)(2,1)} async-done(((bf16[64,85,128]{2,1,0:T(8,128)(2,1)}), bf16[64,85,128]{2,1,0:T(8,128)(2,1)}, u32[]{:S(2)}, u32[]{:S(2)}) %all-to-all-start.1) | async-done | bytes 1392672 | tf_op jit(solution)/shard_map/all_to_all | solution.py:122
  279.0 3.1 %reshape.114 = bf16[320,2176]{1,0:T(8,128)(2,1)S(1)} reshape(bf16[64,85,128]{2,1,0:T(8,128)(2,1)} %all-to-all-done.1) | data formatting | bytes 2785280 | tf_op jit(solution)/shard_map/reshape | solution.py:128
  282.3 2.0 gather_fusion.3
  285.0 1.3 convolution_convert_fusion.2
  (64 shorter events, 4.2 us)
Async XLA Ops:
  7.2 7.3 %copy-start = (bf16[128,2048]{1,0:T(8,128)(2,1)S(1)}, bf16[128,2048]{1,0:T(8,128)(2,1)}, u32[]{:S(2)}) copy-start(bf16[128,2048]{1,0:T(8,128)(2,1)} %param.7) | copy-start | bytes 1572868
  14.5 2.5 copy-start.1
  25.1 141.3 %all-to-all-start = ((bf16[64,160,128]{2,1,0:T(8,128)(2,1)}), bf16[64,160,128]{2,1,0:T(8,128)(2,1)S(1)}, u32[]{:S(2)}, u32[]{:S(2)}) async-start(bf16[64,160,128]{2,1,0:T(8,128)(2,1)} %reshape.111), calls=%async_computation | async-start | bytes 5242880 | tf_op jit(solution)/shard_map/all_to_all | solution.py:75
  43.7 127.8 %all-gather.2.cloned.1.call-start = ((), (), s32[]{:S(2)}) async-start(), calls=%async_computation.3 | async-start | bytes 6553600 | tf_op jit(solution)/shard_map/all_gather | solution.py:84
  169.5 7.0 %collective-permute-start = (bf16[320,4096]{1,0:T(8,128)(2,1)}, bf16[320,4096]{1,0:T(8,128)(2,1)S(1)}, u32[]{:S(2)}, u32[]{:S(2)}) collective-permute-start(bf16[320,4096]{1,0:T(8,128)(2,1)} %reshape.112), channel_id=1, source_target_pairs={{0,4},{4,0},{1,5},{5,1},{2,6},{6,2},{3,7},{7,3},{8,12},{12,8},{9,1... | collective-permute-start | bytes 7864328 | tf_op jit(solution)/shard_map/ppermute | solution.py:83
  171.5 9.0 %copy-start.9 = (bf16[2,2048,640]{1,2,0:T(8,128)(2,1)S(1)}, bf16[2,2048,640]{1,2,0:T(8,128)(2,1)}, u32[]{:S(2)}) copy-start(bf16[2,2048,640]{1,2,0:T(8,128)(2,1)} %all-gather.2.cloned.1.call-done) | copy-start | bytes 15728644
  176.5 3.9 %copy-start.6 = (bf16[320,4096]{1,0:T(8,128)(2,1)}, bf16[320,4096]{1,0:T(8,128)(2,1)S(1)}, u32[]{:S(2)}) copy-start(bf16[320,4096]{1,0:T(8,128)(2,1)S(1)} %collective-permute-done) | copy-start | bytes 7864324
  180.5 1.6 copy-start.4
  183.5 2.5 copy-start.2
  183.6 5.8 %collective-permute-start.1 = (bf16[320,2176]{1,0:T(8,128)(2,1)S(1)}, bf16[320,2176]{1,0:T(8,128)(2,1)S(1)}, u32[]{:S(2)}, u32[]{:S(2)}) collective-permute-start(bf16[320,2176]{1,0:T(8,128)(2,1)S(1)} %pad_maximum_fusion.1), channel_id=1, source_target_pairs={{0,4},{4,0},{1,5},{5,1},{2,6},{6,2},{3,7},{7,3},{8,12},{12,8},{9,1... | collective-permute-start | bytes 4177928 | tf_op jit(solution)/shard_map/ppermute | solution.py:105
  187.3 2.2 copy-start.3
  189.4 1.1 copy-start.8
  200.4 78.6 %all-to-all-start.1 = ((bf16[64,85,128]{2,1,0:T(8,128)(2,1)}), bf16[64,85,128]{2,1,0:T(8,128)(2,1)}, u32[]{:S(2)}, u32[]{:S(2)}) async-start(bf16[64,85,128]{2,1,0:T(8,128)(2,1)} %reshape.113), calls=%async_computation.1 | async-start | bytes 2883584 | tf_op jit(solution)/shard_map/all_to_all | solution.py:122
  206.4 79.9 %reduce-scatter.2.cloned.1.call-start = ((), (), s32[]{:S(2)}) async-start(), calls=%async_computation.4 | async-start | bytes 3276800 | tf_op jit(solution)/shard_map/reduce_scatter | solution.py:94
  206.5 3.0 %copy-start.5 = (f32[320,640]{1,0:T(8,128)S(1)}, f32[320,640]{1,0:T(8,128)}, u32[]{:S(2)}) copy-start(f32[320,640]{1,0:T(8,128)} %copy-done.4) | copy-start | bytes 2457604
  206.5 3.0 %copy-start.7 = (bf16[320,4096]{1,0:T(8,128)(2,1)S(1)}, bf16[320,4096]{1,0:T(8,128)(2,1)}, u32[]{:S(2)}) copy-start(bf16[320,4096]{1,0:T(8,128)(2,1)} %copy-done.6) | copy-start | bytes 7864324
Sparse Core Ops, SparseCore 0:
  48.5 63.6 all-gather.1
  212.8 40.4 reduce-scatter.1

commit v9 on v7

--- a/solution.py
+++ b/solution.py
@@ -74,11 +74,14 @@
     is_valid = where_from >= 0
     assign = jnp.where(is_valid, where_from, 0)
     token_index = assign // 2
-    send_x = jnp.where(is_valid[:, None], tokens[token_index], jnp.zeros((), tokens.dtype))
+    pick = (
+        (token_index[:, None] == jnp.arange(tok_rows, dtype=jnp.int32)[None, :]) & is_valid[:, None]
+    ).astype(jnp.bfloat16)
+    send_x = jnp.dot(pick, tokens, preferred_element_type=jnp.float32).astype(jnp.bfloat16)
     send_gate = jnp.where(is_valid, gate_values.reshape(-1)[assign], 0.0)
-    send_scaled = (send_gate[:, None] * cotangent[token_index].astype(jnp.float32)).astype(
-        jnp.bfloat16
-    )
+    send_scaled = (
+        send_gate[:, None] * jnp.dot(pick, cotangent, preferred_element_type=jnp.float32)
+    ).astype(jnp.bfloat16)
     send = jnp.concatenate([send_x, send_scaled], axis=1)
     row_width = send.shape[1]
     arrived = lax.all_to_all(

time: 291 us -> 285 us (0.979)
  local copies, waits for them, and re-layouts: 32.4 us -> 27.2 us
    gather x2 -> x0, local copies, waits for them, and re-layouts: 4.87 us -> none  [the longest x1 2.44 us: local(): tokens[token_index]]
    unnamed x17 -> x13, local copies, waits for them, and re-layouts: 8.35 us -> 8 us
where the time goes in v9:
time: 285 us
  waiting for transfers between devices  188 us (66%)
  starting transfers between devices  28.8 us (10%)
  local copies, waits for them, and re-layouts  27.2 us (10%)
  matrix products  20.9 us (7%)
  between operations  14.4 us (5%)
  other arithmetic  4.99 us (2%)
    all_to_all x1, waiting for transfers between devices, local(): lax.all_to_all(send.reshape(experts, capacity * row_width // LANES, LANES...  118 us
    all_to_all x1, waiting for transfers between devices, local(): lax.all_to_all(back.reshape(experts, capacity * back_width // LANES, LANE...  66 us
    all_to_all x1, starting transfers between devices, local(): lax.all_to_all(send.reshape(experts, capacity * row_width // LANES, LANES...  18.6 us
    unnamed x13, local copies, waits for them, and re-layouts  8 us
    dot_general x1, matrix products, expert_terms(): lax.dot_general(hidden_bf, rows_scaled, (((0,), (0,)), ((), ())), preferr...  6.04 us
    all_to_all x1, starting transfers between devices, local(): lax.all_to_all(back.reshape(experts, capacity * back_width // LANES, LANE...  5.83 us
  transfers between devices with their start and end apart: 6, of which 4 were waited for; matrix products, arithmetic and copies ran while one was open for 9% of the time, Pallas kernels for 0%

profile of v9, /device:TPU:24, one launch (start us, length us, event | category | flops | bytes accessed | tf_op | source)
XLA Modules:
  0.0 284.6 jit_solution(2872168789875111820)
XLA Ops:
  7.2 0.8 copy.19
  8.3 0.6 reduce-window.6
  9.6 1.4 scatter_custom_fusion
  11.1 0.8 copy.24
  12.0 2.5 gather_fusion
  14.5 0.6 convolution_convert_fusion.2
  15.1 0.6 fusion
  15.8 3.1 %reshape.109 = bf16[64,160,128]{2,1,0:T(8,128)(2,1)} reshape(bf16[320,4096]{1,0:T(8,128)(2,1)S(1)} %pad_maximum_fusion) | data formatting | bytes 5242880 | tf_op jit(solution)/shard_map/reshape | solution.py:88
  18.9 18.6 %all-to-all-start = ((bf16[64,160,128]{2,1,0:T(8,128)(2,1)}), bf16[64,160,128]{2,1,0:T(8,128)(2,1)S(1)}, u32[]{:S(2)}, u32[]{:S(2)}) async-start(bf16[64,160,128]{2,1,0:T(8,128)(2,1)} %reshape.109), calls=%async_computation | async-start | bytes 5242880 | tf_op jit(solution)/shard_map/all_to_all | solution.py:87
  37.6 2.2 copy.25
  39.7 2.5 pad_maximum_fusion.3
  42.2 118.0 %all-to-all-done = bf16[64,160,128]{2,1,0:T(8,128)(2,1)S(1)} async-done(((bf16[64,160,128]{2,1,0:T(8,128)(2,1)}), bf16[64,160,128]{2,1,0:T(8,128)(2,1)S(1)}, u32[]{:S(2)}, u32[]{:S(2)}) %all-to-all-start) | async-done | bytes 2621472 | tf_op jit(solution)/shard_map/all_to_all | solution.py:87
  160.2 3.1 %reshape.110 = bf16[320,4096]{1,0:T(8,128)(2,1)} reshape(bf16[64,160,128]{2,1,0:T(8,128)(2,1)S(1)} %all-to-all-done) | data formatting | bytes 5242880 | tf_op jit(solution)/shard_map/reshape | solution.py:93
  163.3 2.1 collective-permute-start
  165.4 3.5 %constant_dynamic-update-slice_fusion.1 = bf16[640,4096]{1,0:T(8,128)(2,1)} fusion(bf16[320,4096]{1,0:T(8,128)(2,1)} %reshape.110), kind=kLoop, calls=%fused_computation.64 | loop fusion | bytes 5242880
  169.0 1.4 collective-permute-done
  170.3 1.9 constant_dynamic-update-slice_fusion
  172.2 4.9 %fusion.1 = f32[640,640]{0,1:T(8,128)S(1)} fusion(bf16[640,4096]{1,0:T(8,128)(2,1)} %constant_dynamic-update-slice_fusion, bf16[2,2048,640]{1,2,0:T(8,128)(2,1)} %all-gather.2.cloned.1.call-done), kind=kOutput, calls=%fused_computation.9 | convolution fusion | flops 1677721600 | bytes 6881280 | tf_op jit(solution)/shard_map/dot_general | solution.py:39
  177.1 4.7 %multiply_reduce_fusion = (f32[640]{0:T(1024)S(1)}, f32[640,640]{0,1:T(8,128)S(1)}) fusion(f32[640,640]{0,1:T(8,128)S(1)} %fusion.1, bf16[2,2048,640]{1,2,0:T(8,128)(2,1)S(1)} %copy-done.2, bf16[640,4096]{1,0:T(8,128)(2,1)} %constant_dynamic-update-slice_fusion), kind=kOutput, calls=%fused_computation.27 | convolution fusion | flops 1681816960 | bytes 8522240 | tf_op jit(solution)/shard_map/dot_general | solution.py:40
  181.9 2.9 %convolution_convert_fusion.1 = bf16[640,2048]{1,0:T(8,128)(2,1)S(1)} fusion(bf16[2,2048,640]{1,2,0:T(8,128)(2,1)S(1)} %copy-done.2, f32[640,640]{0,1:T(8,128)S(1)} %get-tuple-element.18, f32[640,640]{0,1:T(8,128)S(1)} %fusion.1), kind=kOutput, calls=%fused_computation.4 | convolution fusion | flops 1686814720 | bytes 8519680 | tf_op jit(solution)/shard_map/dot_general | solution.py:53
  185.3 2.0 collective-permute-start.1
  187.3 3.0 %collective-permute-done.1 = bf16[320,2176]{1,0:T(8,128)(2,1)S(1)} collective-permute-done((bf16[320,2176]{1,0:T(8,128)(2,1)S(1)}, bf16[320,2176]{1,0:T(8,128)(2,1)S(1)}, u32[]{:S(2)}, u32[]{:S(2)}) %collective-permute-start.1) | collective-permute-done | bytes 1392672 | tf_op jit(solution)/shard_map/ppermute | solution.py:108
  190.7 0.4 add_convert_fusion
  191.2 2.5 reshape.111
  193.7 5.8 %all-to-all-start.1 = ((bf16[64,85,128]{2,1,0:T(8,128)(2,1)}), bf16[64,85,128]{2,1,0:T(8,128)(2,1)S(1)}, u32[]{:S(2)}, u32[]{:S(2)}) async-start(bf16[64,85,128]{2,1,0:T(8,128)(2,1)} %reshape.111), calls=%async_computation.1 | async-start | bytes 2883584 | tf_op jit(solution)/shard_map/all_to_all | solution.py:125
  199.5 0.3 reduce-scatter.2.cloned.1.call-start
  199.8 6.0 %convolution_convert_fusion = bf16[640,2048]{1,0:T(8,128)(2,1)} fusion(bf16[640,4096]{1,0:T(8,128)(2,1)} %constant_dynamic-update-slice_fusion, f32[640,640]{0,1:T(8,128)} %copy-done.3), kind=kOutput, calls=%fused_computation.3 | convolution fusion | flops 1682718720 | bytes 6881280 | tf_op jit(solution)/shard_map/dot_general | solution.py:44
  206.0 66.0 %all-to-all-done.1 = bf16[64,85,128]{2,1,0:T(8,128)(2,1)S(1)} async-done(((bf16[64,85,128]{2,1,0:T(8,128)(2,1)}), bf16[64,85,128]{2,1,0:T(8,128)(2,1)S(1)}, u32[]{:S(2)}, u32[]{:S(2)}) %all-to-all-start.1) | async-done | bytes 1392672 | tf_op jit(solution)/shard_map/all_to_all | solution.py:125
  272.0 1.6 reshape.112
  273.8 2.0 gather_fusion.1
  275.9 0.6 copy.27
  276.5 1.3 convolution_convert_fusion.3
  (47 shorter events, 2.8 us)
Async XLA Ops:
  7.2 7.3 %copy-start = (bf16[128,2048]{1,0:T(8,128)(2,1)S(1)}, bf16[128,2048]{1,0:T(8,128)(2,1)}, u32[]{:S(2)}) copy-start(bf16[128,2048]{1,0:T(8,128)(2,1)} %param.6) | copy-start | bytes 1572868
  12.0 3.1 %copy-start.1 = (bf16[128,2048]{1,0:T(8,128)(2,1)S(1)}, bf16[128,2048]{1,0:T(8,128)(2,1)}, u32[]{:S(2)}) copy-start(bf16[128,2048]{1,0:T(8,128)(2,1)} %param.7) | copy-start | bytes 1572868
  18.9 141.3 %all-to-all-start = ((bf16[64,160,128]{2,1,0:T(8,128)(2,1)}), bf16[64,160,128]{2,1,0:T(8,128)(2,1)S(1)}, u32[]{:S(2)}, u32[]{:S(2)}) async-start(bf16[64,160,128]{2,1,0:T(8,128)(2,1)} %reshape.109), calls=%async_computation | async-start | bytes 5242880 | tf_op jit(solution)/shard_map/all_to_all | solution.py:87
  37.5 134.7 %all-gather.2.cloned.1.call-start = ((), (), s32[]{:S(2)}) async-start(), calls=%async_computation.3 | async-start | bytes 6553600 | tf_op jit(solution)/shard_map/all_gather | solution.py:35
  163.3 7.0 %collective-permute-start = (bf16[320,4096]{1,0:T(8,128)(2,1)}, bf16[320,4096]{1,0:T(8,128)(2,1)S(1)}, u32[]{:S(2)}, u32[]{:S(2)}) collective-permute-start(bf16[320,4096]{1,0:T(8,128)(2,1)} %reshape.110), channel_id=1, source_target_pairs={{0,4},{4,0},{1,5},{5,1},{2,6},{6,2},{3,7},{7,3},{8,12},{12,8},{9,1... | collective-permute-start | bytes 7864328 | tf_op jit(solution)/shard_map/ppermute | solution.py:95
  172.2 4.9 %copy-start.2 = (bf16[2,2048,640]{1,2,0:T(8,128)(2,1)S(1)}, bf16[2,2048,640]{1,2,0:T(8,128)(2,1)}, u32[]{:S(2)}) copy-start(bf16[2,2048,640]{1,2,0:T(8,128)(2,1)} %all-gather.2.cloned.1.call-done) | copy-start | bytes 15728644
  177.1 4.7 %copy-start.3 = (f32[640,640]{0,1:T(8,128)}, f32[640,640]{0,1:T(8,128)S(1)}, u32[]{:S(2)}) copy-start(f32[640,640]{0,1:T(8,128)S(1)} %fusion.1) | copy-start | bytes 4915204
  185.3 5.0 %collective-permute-start.1 = (bf16[320,2176]{1,0:T(8,128)(2,1)S(1)}, bf16[320,2176]{1,0:T(8,128)(2,1)S(1)}, u32[]{:S(2)}, u32[]{:S(2)}) collective-permute-start(bf16[320,2176]{1,0:T(8,128)(2,1)S(1)} %pad_maximum_fusion.1), channel_id=1, source_target_pairs={{0,4},{4,0},{1,5},{5,1},{2,6},{6,2},{3,7},{7,3},{8,12},{12,8},{9,1... | collective-permute-start | bytes 4177928 | tf_op jit(solution)/shard_map/ppermute | solution.py:108
  193.7 78.3 %all-to-all-start.1 = ((bf16[64,85,128]{2,1,0:T(8,128)(2,1)}), bf16[64,85,128]{2,1,0:T(8,128)(2,1)S(1)}, u32[]{:S(2)}, u32[]{:S(2)}) async-start(bf16[64,85,128]{2,1,0:T(8,128)(2,1)} %reshape.111), calls=%async_computation.1 | async-start | bytes 2883584 | tf_op jit(solution)/shard_map/all_to_all | solution.py:125
  199.5 78.3 %reduce-scatter.2.cloned.1.call-start = ((), (), s32[]{:S(2)}) async-start(), calls=%async_computation.4 | async-start | bytes 3276800 | tf_op jit(solution)/shard_map/reduce_scatter | solution.py:48
Sparse Core Ops, SparseCore 0:
  42.3 63.6 all-gather.1
  206.0 40.5 reduce-scatter.1
